TPU v7x, 32 devices: a whole 2x2x4 slice. The times are simulated.
32 devices in a mesh: seq: 16 (over z, y, core), fsdp: 2 (over x).
Axes of the slice: x: 2, y: 2, z: 4, core: 2. Of those that a mesh axis runs over, the one named last changes fastest.
Arguments:
- queries: bfloat16 [2, 8192, 1024], P('fsdp', 'seq'), may hold values from -10.5 to 10.5
- key_vectors: bfloat16 [2, 8192, 1024], P('fsdp', 'seq'), may hold values from -10.5 to 10.5
- value_vectors: bfloat16 [2, 8192, 1024], P('fsdp', 'seq'), may hold values from -6 to 6
- grad_mixed: bfloat16 [2, 8192, 2048], P('fsdp', 'seq'), may hold values from -24 to 24
- out_weight: bfloat16 [1024, 2048], P('fsdp'), may hold values from -0.1875 to 0.1875
- head_phase: int32 [8], replicated, may hold values from 0 to 3
- segments_short: int32 [7], replicated, may hold values from 1 to 2048, 8192 in all
- segments_long: int32 [1], replicated, may hold values from 1 to 8192, as said below
Outputs:
- grad_query: bfloat16 [2, 8192, 1024], P('fsdp', 'seq')
- grad_key: bfloat16 [2, 8192, 1024], P('fsdp', 'seq')
- grad_value: bfloat16 [2, 8192, 1024], P('fsdp', 'seq')
Inputs may be any that keep to these rules, and one draw needn't show every extreme that they name: `segments_long`: lengths that sum to 8192; the last of them is 8192, the others are shorter.
All inputs are finite; a program needn't handle non-finite values.
Results may differ from a plain program's by a relative error of at most 0.0095.
Values may be sent and summed in bfloat16 or wider, within the bound.
No kernel may reach another device: no remote copies, remote signals or barrier semaphores. Data moves between devices by JAX's collectives and lax.ppermute only.
A program may use at most 256 MiB of HBM per device.

v0:
```python
import functools
import math

import jax
import jax.numpy as jnp
from jax import lax
from jax.experimental import pallas as pl
from jax.experimental.pallas import tpu as pltpu
from jax.sharding import PartitionSpec as P


REACH_SHORT = 4


VERY_NEGATIVE = -1e30


def passed_along(value, axis, by):
    devices = lax.axis_size(axis)
    pairs = [(i, i + by) for i in range(devices) if 0 <= i + by < devices]
    return lax.ppermute(value, axis, pairs)


def take_rows(tensor, parity):
    layout = tensor.shape
    paired = tensor.reshape(layout[:-2] + (layout[-2] // 2, 2, layout[-1]))
    return jnp.where((parity == 0)[:, None, None], paired[..., 0, :], paired[..., 1, :])


def put_rows(tensor, parity):
    zero_fill = jnp.zeros_like(tensor)
    first_half = jnp.where((parity == 0)[:, None, None], tensor, zero_fill)
    second_half = jnp.where((parity == 1)[:, None, None], tensor, zero_fill)
    stacked = jnp.stack([first_half, second_half], axis=-2)
    return stacked.reshape(tensor.shape[:-2] + (2 * tensor.shape[-2], tensor.shape[-1]))


def take_stats(tensor, parity):
    paired = tensor.reshape(tensor.shape[:-1] + (tensor.shape[-1] // 2, 2))
    return jnp.where((parity == 0)[:, None, None], paired[..., 0], paired[..., 1])


def segment_of(positions, lengths):
    seg_ends = jnp.cumsum(lengths)
    return jnp.sum((positions[..., None] >= seg_ends).astype(jnp.int32), axis=-1)


def row_positions(shard_index, tok_dev, stride, offset, row_count):
    return (
        shard_index * tok_dev
        + stride * jnp.arange(row_count, dtype=jnp.int32)[None, :]
        + offset[:, None]
    )


def window_positions(shard_index, distances, tok_dev, stride, offset, row_count):
    return jnp.concatenate(
        [row_positions(shard_index + d, tok_dev, stride, offset, row_count) for d in distances],
        axis=1,
    )


def dot_nt(left, right):
    return lax.dot_general(
        left, right, (((1,), (1,)), ((), ())), preferred_element_type=jnp.float32
    )


def dot_nn(left, right):
    return lax.dot_general(
        left, right, (((1,), (0,)), ((), ())), preferred_element_type=jnp.float32
    )


def query_kernel(
    q_ref, g_ref, ks_ref, vs_ref, kl_ref, vl_ref,
    qpos_ref, qss_ref, qsl_ref, kps_ref, kss_ref, kpl_ref, ksl_ref,
    dq_ref, top_ref, inv_ref, delta_ref, *, scale,
):
    q = q_ref[0]
    g = g_ref[0]
    qpos = qpos_ref[0]
    parts = []
    for k_ref, v_ref, kp_ref, kseg_ref, qseg_ref in (
        (ks_ref, vs_ref, kps_ref, kss_ref, qss_ref),
        (kl_ref, vl_ref, kpl_ref, ksl_ref, qsl_ref),
    ):
        k = k_ref[0]
        live = (kp_ref[0] <= qpos) & (kseg_ref[0] == qseg_ref[0])
        scores = jnp.where(live, dot_nt(q, k) * scale, VERY_NEGATIVE)
        parts.append((live, scores, k, v_ref))
    top = jnp.maximum(
        jnp.max(parts[0][1], axis=1, keepdims=True), jnp.max(parts[1][1], axis=1, keepdims=True)
    )
    total = None
    numer = None
    weights = []
    for live, scores, k, v_ref in parts:
        w = jnp.where(live, jnp.exp(scores - top), 0.0)
        part_total = jnp.sum(w, axis=1, keepdims=True)
        part_numer = dot_nn(w.astype(jnp.bfloat16), v_ref[0])
        total = part_total if total is None else total + part_total
        numer = part_numer if numer is None else numer + part_numer
        weights.append(w)
    attended = numer / total
    delta = jnp.sum(g.astype(jnp.float32) * attended, axis=1, keepdims=True)
    inverse = 1.0 / total
    grad_query = None
    for (live, scores, k, v_ref), w in zip(parts, weights):
        probability = w * inverse
        grad_probs = dot_nt(g, v_ref[0])
        grad_scores = (probability * (grad_probs - delta)).astype(jnp.bfloat16)
        part = dot_nn(grad_scores, k) * scale
        grad_query = part if grad_query is None else grad_query + part
    dq_ref[0] = grad_query
    top_ref[0] = top
    inv_ref[0] = inverse
    delta_ref[0] = delta


def key_kernel(
    k_ref, v_ref, qs_ref, gs_ref, ql_ref, gl_ref,
    kpos_ref, kss_ref, ksl_ref, qps_ref, qss_ref, sts_ref, qpl_ref, qsl_ref, stl_ref,
    dk_ref, dv_ref, *, scale,
):
    k = k_ref[0]
    v = v_ref[0]
    kpos = kpos_ref[0]
    grad_key = None
    grad_value = None
    for q_ref, g_ref, qp_ref, qseg_ref, kseg_ref, st_ref in (
        (qs_ref, gs_ref, qps_ref, qss_ref, kss_ref, sts_ref),
        (ql_ref, gl_ref, qpl_ref, qsl_ref, ksl_ref, stl_ref),
    ):
        q = q_ref[0]
        g = g_ref[0]
        live = (kpos <= qp_ref[0]) & (kseg_ref[0] == qseg_ref[0])
        scores = jnp.where(live, dot_nt(k, q) * scale, VERY_NEGATIVE)
        stats = st_ref[0]
        probability = jnp.where(live, jnp.exp(scores - stats[0:1, :]), 0.0) * stats[1:2, :]
        grad_probs = dot_nt(v, g)
        grad_scores = (probability * (grad_probs - stats[2:3, :])).astype(jnp.bfloat16)
        part_key = dot_nn(grad_scores, q) * scale
        part_value = dot_nn(probability.astype(jnp.bfloat16), g)
        grad_key = part_key if grad_key is None else grad_key + part_key
        grad_value = part_value if grad_value is None else grad_value + part_value
    dk_ref[0] = grad_key
    dv_ref[0] = grad_value


def per_head(shape):
    return pl.BlockSpec((1,) + tuple(shape[1:]), lambda h: (h,) + (0,) * (len(shape) - 1))


def run_per_head(kernel, inputs, out_shapes):
    heads = inputs[0].shape[0]
    return pl.pallas_call(
        kernel,
        grid=(heads,),
        in_specs=[per_head(x.shape) for x in inputs],
        out_specs=[per_head(s.shape) for s in out_shapes],
        out_shape=out_shapes,
        compiler_params=pltpu.CompilerParams(dimension_semantics=("arbitrary",)),
    )(*inputs)


def column(x):
    return x[:, :, None]


def row(x):
    return x[:, None, :]


def shards(
    queries,
    key_vectors,
    value_vectors,
    grad_mixed,
    out_weight,
    head_phase,
    segments_short,
    segments_long,
):
    shard_index = lax.axis_index("seq")
    devices = lax.axis_size("seq")
    tok_dev = queries.shape[1]
    total = devices * tok_dev
    head_count = head_phase.shape[0]
    head_width = queries.shape[2] // head_count
    rows_short = tok_dev // 2
    rows_long = tok_dev // 4
    scale = 1.0 / math.sqrt(head_width)
    par_short = head_phase % 2
    par_long = head_phase // 2

    def split_rows(tensor):
        heads_major = jnp.transpose(tensor.reshape(tok_dev, head_count, head_width), (1, 0, 2))
        return take_rows(heads_major, par_short)

    def gathered(tensor):
        return lax.all_gather(tensor, "seq", axis=2, tiled=True)

    near_steps = [d for d in range(1, REACH_SHORT + 1) if d < devices]
    long_pos = row_positions(0, tok_dev, 4, head_phase, devices * rows_long)
    long_seg = segment_of(long_pos, segments_long)

    own_kv = jnp.stack([split_rows(key_vectors[0]), split_rows(value_vectors[0])])
    all_kv_long = gathered(take_rows(own_kv, par_long))
    near_kv = [own_kv] + [passed_along(own_kv, "seq", d) for d in near_steps]
    near_kv = jnp.concatenate(near_kv, axis=2)

    q_rows = split_rows(queries[0])
    core = shard_index % 2
    half_width = out_weight.shape[1] // 2
    own_half = lax.all_gather(
        lax.dynamic_slice_in_dim(out_weight, core * half_width, half_width, axis=1),
        "fsdp",
        axis=0,
        tiled=True,
    )
    other_half = lax.ppermute(own_half, "seq", [(i, i ^ 1) for i in range(devices)])
    grad_out = jnp.einsum(
        "td,rd->tr",
        lax.dynamic_slice_in_dim(grad_mixed[0], core * half_width, half_width, axis=1),
        own_half,
        preferred_element_type=jnp.float32,
    ) + jnp.einsum(
        "td,rd->tr",
        lax.dynamic_slice_in_dim(grad_mixed[0], (1 - core) * half_width, half_width, axis=1),
        other_half,
        preferred_element_type=jnp.float32,
    )
    grad_out = grad_out.astype(jnp.bfloat16)
    g_rows = split_rows(grad_out)
    own_qg = jnp.stack([q_rows, g_rows])
    all_qg_long = gathered(take_rows(own_qg, par_long))
    near_qg = [own_qg] + [passed_along(own_qg, "seq", -d) for d in near_steps]
    near_qg = jnp.concatenate(near_qg, axis=2)

    own_pos = row_positions(shard_index, tok_dev, 2, par_short, rows_short)
    own_seg_short = segment_of(own_pos, segments_short)
    own_is_long = (own_pos - head_phase[:, None]) % 4 == 0
    own_seg_long = jnp.where(own_is_long, segment_of(own_pos, segments_long), -3)

    key_pos_short = window_positions(
        shard_index, [-d for d in range(len(near_steps) + 1)], tok_dev, 2, par_short, rows_short
    )
    key_seg_short = jnp.where(key_pos_short >= 0, segment_of(key_pos_short, segments_short), -1)
    f32 = jnp.float32
    row_shape = jax.ShapeDtypeStruct((head_count, rows_short, head_width), f32)
    stat_shape = jax.ShapeDtypeStruct((head_count, rows_short, 1), f32)
    grad_query, top, inverse, delta = run_per_head(
        functools.partial(query_kernel, scale=scale),
        [
            q_rows,
            g_rows,
            near_kv[0],
            near_kv[1],
            all_kv_long[0],
            all_kv_long[1],
            column(own_pos),
            column(own_seg_short),
            column(own_seg_long),
            row(key_pos_short),
            row(key_seg_short),
            row(long_pos),
            row(long_seg),
        ],
        [row_shape, stat_shape, stat_shape, stat_shape],
    )
    own_stats = jnp.stack([top[:, :, 0], inverse[:, :, 0], delta[:, :, 0]], axis=1)
    near_stats = [own_stats] + [passed_along(own_stats, "seq", -d) for d in near_steps]
    near_stats = jnp.concatenate(near_stats, axis=2)
    all_stats_long = lax.all_gather(take_stats(own_stats, par_long), "seq", axis=2, tiled=True)

    query_pos_short = window_positions(
        shard_index, list(range(len(near_steps) + 1)), tok_dev, 2, par_short, rows_short
    )
    query_seg_short = jnp.where(
        query_pos_short < total, segment_of(query_pos_short, segments_short), -2
    )
    grad_key, grad_value = run_per_head(
        functools.partial(key_kernel, scale=scale),
        [
            own_kv[0],
            own_kv[1],
            near_qg[0],
            near_qg[1],
            all_qg_long[0],
            all_qg_long[1],
            column(own_pos),
            column(own_seg_short),
            column(own_seg_long),
            row(query_pos_short),
            row(query_seg_short),
            near_stats,
            row(long_pos),
            row(long_seg),
            all_stats_long,
        ],
        [row_shape, row_shape],
    )

    def to_tokens(rows_here):
        tokens = put_rows(rows_here.astype(jnp.bfloat16), par_short)
        return jnp.transpose(tokens, (1, 0, 2)).reshape(1, tok_dev, head_count * head_width)

    return (to_tokens(grad_query), to_tokens(grad_key), to_tokens(grad_value))


def solution(mesh):
    placed = (
        P("fsdp", "seq", None),
        P("fsdp", "seq", None),
        P("fsdp", "seq", None),
        P("fsdp", "seq", None),
        P("fsdp", None),
        P(),
        P(),
        P(),
    )

    return jax.shard_map(
        shards,
        mesh=mesh,
        in_specs=placed,
        out_specs=(P("fsdp", "seq", None), P("fsdp", "seq", None), P("fsdp", "seq", None)),
        check_vma=False,
    )
```

profile of v0, /device:TPU:5, one launch (start us, length us, event | category | flops | bytes accessed | tf_op | source)
XLA Modules:
  0.0 401.1 jit_solution(6410476843867038739)
XLA Ops:
  7.3 2.5 constant_dynamic-slice_fusion
  9.8 34.5 %all-gather.4.cloned.1.call-done = bf16[1024,1024]{1,0:T(8,128)(2,1)} async-done(((bf16[512,1024]{1,0:T(8,128)(2,1)}), bf16[1024,1024]{1,0:T(8,128)(2,1)}) %all-gather.4.cloned.1.call-update) | async-done | bytes 2097168 | tf_op jit(solution)/shard_map/all_gather | solution.py:216
  45.1 2.6 copy.178
  52.4 2.9 fusion.4
  55.3 3.0 fusion
  66.5 2.3 bitcast_select_fusion.1
  68.8 1.8 pad_maximum_fusion
  70.6 3.0 collective-permute-start.1
  73.6 3.1 collective-permute-start.2
  76.7 2.7 collective-permute-start.3
  80.8 1.8 convert_select_fusion
  83.2 4.1 %collective-permute-start.4 = (bf16[2,8,256,128]{3,2,1,0:T(8,128)(2,1)}, bf16[2,8,256,128]{3,2,1,0:T(8,128)(2,1)}, u32[]{:S(2)}, u32[]{:S(2)}) collective-permute-start(bf16[2,8,256,128]{3,2,1,0:T(8,128)(2,1)} %get-tuple-element.35), channel_id=1, source_target_pairs={{0,8},{2,10},{4,12},{6,14},{8,16},{10,18},{12,20},{14,22},{16,24},... | collective-permute-start | bytes 3145736 | tf_op jit(solution)/shard_map/ppermute | solution.py:21
  87.3 1.8 pad_maximum_fusion.2
  89.2 3.0 collective-permute-start.5
  92.2 1.4 copy.125.qss_ref.kss_ref
  94.3 17.1 %collective-permute-done.1 = bf16[2,8,256,128]{3,2,1,0:T(8,128)(2,1)} collective-permute-done((bf16[2,8,256,128]{3,2,1,0:T(8,128)(2,1)}, bf16[2,8,256,128]{3,2,1,0:T(8,128)(2,1)}, u32[]{:S(2)}, u32[]{:S(2)}) %collective-permute-start.1) | collective-permute-done | bytes 1048608 | tf_op jit(solution)/shard_map/ppermute | solution.py:21
  111.3 1.9 collective-permute-start.6
  113.2 64.1 %collective-permute-done.2 = bf16[2,8,256,128]{3,2,1,0:T(8,128)(2,1)} collective-permute-done((bf16[2,8,256,128]{3,2,1,0:T(8,128)(2,1)}, bf16[2,8,256,128]{3,2,1,0:T(8,128)(2,1)}, u32[]{:S(2)}, u32[]{:S(2)}) %collective-permute-start.2) | collective-permute-done | bytes 1048608 | tf_op jit(solution)/shard_map/ppermute | solution.py:21
  177.3 1.9 collective-permute-start.7
  179.2 1.5 collective-permute-start.8
  180.7 3.5 bitcast_select_fusion.2
  184.3 1.5 constant_dynamic-update-slice_fusion.3
  185.8 1.4 constant_dynamic-update-slice_fusion.2
  187.2 1.4 constant_dynamic-update-slice_fusion.1
  188.6 12.0 %collective-permute-done.4 = bf16[2,8,256,128]{3,2,1,0:T(8,128)(2,1)} collective-permute-done((bf16[2,8,256,128]{3,2,1,0:T(8,128)(2,1)}, bf16[2,8,256,128]{3,2,1,0:T(8,128)(2,1)}, u32[]{:S(2)}, u32[]{:S(2)}) %collective-permute-start.4) | collective-permute-done | bytes 1048608 | tf_op jit(solution)/shard_map/ppermute | solution.py:21
  200.5 1.5 constant_dynamic-update-slice_fusion
  202.1 1.4 constant_dynamic-update-slice_fusion.18
  203.6 10.0 %collective-permute-done.7 = bf16[2,8,256,128]{3,2,1,0:T(8,128)(2,1)S(1)} collective-permute-done((bf16[2,8,256,128]{3,2,1,0:T(8,128)(2,1)}, bf16[2,8,256,128]{3,2,1,0:T(8,128)(2,1)S(1)}, u32[]{:S(2)}, u32[]{:S(2)}) %collective-permute-start.7) | collective-permute-done | bytes 1048608 | tf_op jit(solution)/shard_map/ppermute | solution.py:21
  214.9 2.7 slice_bitcast_fusion.6
  217.6 2.8 slice_bitcast_fusion.4
  220.5 5.9 %slice_bitcast_fusion.2 = (bf16[8,2048,128]{2,1,0:T(8,128)(2,1)}, bf16[8,2048,128]{2,1,0:T(8,128)(2,1)}) fusion(bf16[2,8,2048,128]{3,2,1,0:T(8,128)(2,1)} %all-gather.6.cloned.1.call-done), kind=kLoop, calls=%fused_computation.2 | loop fusion | bytes 16777216 | tf_op jit(solution)/shard_map/squeeze | solution.py:261
  226.3 29.5 %shard_map.103 = (f32[8,256,128]{2,1,0:T(8,128)}, f32[8,256,1]{2,1,0:T(8,128)}, f32[8,256,1]{2,1,0:T(8,128)}, f32[8,256,1]{2,1,0:T(8,128)}) custom-call(bf16[8,256,128]{2,1,0:T(8,128)(2,1)} %get-tuple-element.78.q_ref, bf16[8,256,128]{2,1,0:T(8,128)(2,1)} %get-tuple-element.76.g_ref, bf16[8,1280,128]{2,1,0:T(8,128)(2,1)} %get-tuple-element.26.ks_ref, ...), custom_call_target="tpu_custom_call" | custom-call | tf_op jit(solution)/shard_map/pallas_call | solution.py:157
  255.8 2.9 copy.144
  258.7 2.8 copy.145
  261.5 1.6 reduce
  263.0 1.6 reduce.1
  264.6 1.6 copy.146
  266.6 30.3 %collective-permute-start.9 = (f32[8,3,256]{2,1,0:T(4,128)S(1)}, f32[8,3,256]{2,1,0:T(4,128)S(1)}, u32[]{:S(2)}, u32[]{:S(2)}) collective-permute-start(f32[8,3,256]{2,1,0:T(4,128)S(1)} %get-tuple-element.45), channel_id=1, source_target_pairs={{2,0},{4,2},{6,4},{8,6},{10,8},{12,10},{14,12},{16,14},{18,16},{20... | collective-permute-start | bytes 73736 | tf_op jit(solution)/shard_map/ppermute | solution.py:21
  297.0 21.2 %collective-permute-start.10 = (f32[8,3,256]{2,1,0:T(4,128)S(1)}, f32[8,3,256]{2,1,0:T(4,128)S(1)}, u32[]{:S(2)}, u32[]{:S(2)}) collective-permute-start(f32[8,3,256]{2,1,0:T(4,128)S(1)} %get-tuple-element.45), channel_id=1, source_target_pairs={{4,0},{6,2},{8,4},{10,6},{12,8},{14,10},{16,12},{18,14},{20,16},{2... | collective-permute-start | bytes 73736 | tf_op jit(solution)/shard_map/ppermute | solution.py:21
  318.2 1.9 collective-permute-start.11
  320.1 1.3 collective-permute-start.12
  321.8 5.8 %slice_bitcast_fusion = (bf16[8,2048,128]{2,1,0:T(8,128)(2,1)}, bf16[8,2048,128]{2,1,0:T(8,128)(2,1)}) fusion(bf16[2,8,2048,128]{3,2,1,0:T(8,128)(2,1)} %all-gather.8.cloned.1.call-done), kind=kLoop, calls=%fused_computation | loop fusion | bytes 16777216 | tf_op jit(solution)/shard_map/squeeze | solution.py:291
  327.6 30.2 %all_gather.15.stl_ref = f32[8,3,2048]{2,1,0:T(4,128)} all-gather(f32[8,3,128]{2,1,0:T(4,128)S(1)} %fusion.17), channel_id=1, replica_groups=mesh['seq'=16,'fsdp'=2] {'seq'}, dimensions={2}, use_global_device_ids=true | all-gather | bytes 208896 | tf_op jit(solution)/shard_map/all_gather | solution.py:275
  358.5 25.8 %shard_map.104 = (f32[8,256,128]{2,1,0:T(8,128)}, f32[8,256,128]{2,1,0:T(8,128)}) custom-call(bf16[8,256,128]{2,1,0:T(8,128)(2,1)} %get-tuple-element.77.k_ref, bf16[8,256,128]{2,1,0:T(8,128)(2,1)} %get-tuple-element.75.v_ref, bf16[8,1280,128]{2,1,0:T(8,128)(2,1)} %get-tuple-element.24.qs_ref, bf16[8,1280,128]{2,1,0:T(8,128)(2,1)} %get-tuple-element.23.gs_ref, ...), custom_call_target="tpu_custom_call" | custom-call | tf_op jit(solution)/shard_map/pallas_call | solution.py:157
  384.3 2.8 select_bitcast_fusion.5
  387.9 1.3 reshape.922
  390.0 1.3 reshape.920
  391.3 1.3 pad_maximum_fusion.1
  (143 shorter events, 22.0 us)
Async XLA Ops:
  7.2 45.2 %copy-start = (bf16[1,512,2048]{2,1,0:T(8,128)(2,1)S(1)}, bf16[1,512,2048]{2,1,0:T(8,128)(2,1)}, u32[]{:S(2)}) copy-start(bf16[1,512,2048]{2,1,0:T(8,128)(2,1)} %param.11) | copy-start | bytes 6291460
  7.2 40.5 %copy-start.15 = (bf16[1,512,1024]{2,1,0:T(8,128)(2,1)S(1)}, bf16[1,512,1024]{2,1,0:T(8,128)(2,1)}, u32[]{:S(2)}) copy-start(bf16[1,512,1024]{2,1,0:T(8,128)(2,1)} %param.9) | copy-start | bytes 3145732
  7.2 37.1 %all-gather.4.cloned.1.call-start = ((), (), s32[]{:S(2)}) async-start(), calls=%async_computation | async-start | bytes 3145728 | tf_op jit(solution)/shard_map/all_gather | solution.py:216
  9.7 210.7 %all-gather.6.cloned.1.call-start = ((), (), s32[]{:S(2)}) async-start(), calls=%async_computation.1 | async-start | bytes 8912896 | tf_op jit(solution)/shard_map/all_gather | solution.py:202
  44.3 11.0 %collective-permute-start = (bf16[1024,1024]{1,0:T(8,128)(2,1)}, bf16[1024,1024]{1,0:T(8,128)(2,1)}, u32[]{:S(2)}, u32[]{:S(2)}) collective-permute-start(bf16[1024,1024]{1,0:T(8,128)(2,1)} %all-gather.4.cloned.1.call-done), channel_id=1, source_target_pairs={{0,2},{2,0},{4,6},{6,4},{8,10},{10,8},{12,14},{14,12},{16,18},{18,... | collective-permute-start | bytes 6291464 | tf_op jit(solution)/shard_map/ppermute | solution.py:222
  45.1 2.8 copy-start.16
  48.2 4.1 %copy-start.19 = (s32[8]{0:T(128)S(1)}, s32[8]{0:T(128)}, u32[]{:S(2)}) copy-start(s32[8]{0:T(128)} %param.13) | copy-start | bytes 100
  48.6 1.9 copy-start.4
  48.6 2.8 copy-start.2
  55.3 3.3 copy-start.10
  58.6 1.4 copy-start.11
  58.6 1.4 copy-start.12
  58.6 1.5 copy-start.13
  58.6 1.9 copy-start.14
  59.0 0.8 copy-start.6
  59.0 1.0 copy-start.7
  60.5 2.6 copy-start.20
  60.5 6.0 %copy-start.3 = (bf16[8,256,1,128]{3,0,2,1:T(8,128)(2,1)S(1)}, bf16[8,256,1,128]{3,0,2,1:T(8,128)(2,1)}, u32[]{:S(2)}) copy-start(bf16[8,256,1,128]{3,0,2,1:T(8,128)(2,1)} %copy-done.2) | copy-start | bytes 1572868
  60.5 6.0 %copy-start.5 = (bf16[8,256,1,128]{3,0,2,1:T(8,128)(2,1)S(1)}, bf16[8,256,1,128]{3,0,2,1:T(8,128)(2,1)}, u32[]{:S(2)}) copy-start(bf16[8,256,1,128]{3,0,2,1:T(8,128)(2,1)} %copy-done.4) | copy-start | bytes 1572868
  62.2 259.6 %all-gather.8.cloned.1.call-start = ((), (), s32[]{:S(2)}) async-start(), calls=%async_computation.2 | async-start | bytes 8912896 | tf_op jit(solution)/shard_map/all_gather | solution.py:202
  70.6 40.7 %collective-permute-start.1 = (bf16[2,8,256,128]{3,2,1,0:T(8,128)(2,1)}, bf16[2,8,256,128]{3,2,1,0:T(8,128)(2,1)}, u32[]{:S(2)}, u32[]{:S(2)}) collective-permute-start(bf16[2,8,256,128]{3,2,1,0:T(8,128)(2,1)} %get-tuple-element.35), channel_id=1, source_target_pairs={{0,2},{2,4},{4,6},{6,8},{8,10},{10,12},{12,14},{14,16},{16,18},{18... | collective-permute-start | bytes 3145736 | tf_op jit(solution)/shard_map/ppermute | solution.py:21
  73.6 103.7 %collective-permute-start.2 = (bf16[2,8,256,128]{3,2,1,0:T(8,128)(2,1)}, bf16[2,8,256,128]{3,2,1,0:T(8,128)(2,1)}, u32[]{:S(2)}, u32[]{:S(2)}) collective-permute-start(bf16[2,8,256,128]{3,2,1,0:T(8,128)(2,1)} %get-tuple-element.35), channel_id=1, source_target_pairs={{0,4},{2,6},{4,8},{6,10},{8,12},{10,14},{12,16},{14,18},{16,20},{1... | collective-permute-start | bytes 3145736 | tf_op jit(solution)/shard_map/ppermute | solution.py:21
  76.7 102.5 %collective-permute-start.3 = (bf16[2,8,256,128]{3,2,1,0:T(8,128)(2,1)}, bf16[2,8,256,128]{3,2,1,0:T(8,128)(2,1)}, u32[]{:S(2)}, u32[]{:S(2)}) collective-permute-start(bf16[2,8,256,128]{3,2,1,0:T(8,128)(2,1)} %get-tuple-element.35), channel_id=1, source_target_pairs={{0,6},{2,8},{4,10},{6,12},{8,14},{10,16},{12,18},{14,20},{16,22},{... | collective-permute-start | bytes 3145736 | tf_op jit(solution)/shard_map/ppermute | solution.py:21
  83.2 117.3 %collective-permute-start.4 = (bf16[2,8,256,128]{3,2,1,0:T(8,128)(2,1)}, bf16[2,8,256,128]{3,2,1,0:T(8,128)(2,1)}, u32[]{:S(2)}, u32[]{:S(2)}) collective-permute-start(bf16[2,8,256,128]{3,2,1,0:T(8,128)(2,1)} %get-tuple-element.35), channel_id=1, source_target_pairs={{0,8},{2,10},{4,12},{6,14},{8,16},{10,18},{12,20},{14,22},{16,24},... | collective-permute-start | bytes 3145736 | tf_op jit(solution)/shard_map/ppermute | solution.py:21
  89.2 112.9 %collective-permute-start.5 = (bf16[2,8,256,128]{3,2,1,0:T(8,128)(2,1)}, bf16[2,8,256,128]{3,2,1,0:T(8,128)(2,1)}, u32[]{:S(2)}, u32[]{:S(2)}) collective-permute-start(bf16[2,8,256,128]{3,2,1,0:T(8,128)(2,1)} %get-tuple-element.31), channel_id=1, source_target_pairs={{2,0},{4,2},{6,4},{8,6},{10,8},{12,10},{14,12},{16,14},{18,16},{20... | collective-permute-start | bytes 3145736 | tf_op jit(solution)/shard_map/ppermute | solution.py:21
  93.6 90.7 %copy-start.8 = (bf16[2,8,1280,128]{3,2,1,0:T(8,128)(2,1)S(1)}, bf16[2,8,1280,128]{3,2,1,0:T(8,128)(2,1)}, u32[]{:S(2)}) copy-start(bf16[2,8,1280,128]{3,2,1,0:T(8,128)(2,1)} %get-tuple-element.36) | copy-start | bytes 15728644
  111.3 92.2 %collective-permute-start.6 = (bf16[2,8,256,128]{3,2,1,0:T(8,128)(2,1)}, bf16[2,8,256,128]{3,2,1,0:T(8,128)(2,1)S(1)}, u32[]{:S(2)}, u32[]{:S(2)}) collective-permute-start(bf16[2,8,256,128]{3,2,1,0:T(8,128)(2,1)} %get-tuple-element.31), channel_id=1, source_target_pairs={{4,0},{6,2},{8,4},{10,6},{12,8},{14,10},{16,12},{18,14},{20,16},{2... | collective-permute-start | bytes 3145736 | tf_op jit(solution)/shard_map/ppermute | solution.py:21
  177.3 36.4 %collective-permute-start.7 = (bf16[2,8,256,128]{3,2,1,0:T(8,128)(2,1)}, bf16[2,8,256,128]{3,2,1,0:T(8,128)(2,1)S(1)}, u32[]{:S(2)}, u32[]{:S(2)}) collective-permute-start(bf16[2,8,256,128]{3,2,1,0:T(8,128)(2,1)} %get-tuple-element.31), channel_id=1, source_target_pairs={{6,0},{8,2},{10,4},{12,6},{14,8},{16,10},{18,12},{20,14},{22,16},{... | collective-permute-start | bytes 3145736 | tf_op jit(solution)/shard_map/ppermute | solution.py:21
  179.2 35.5 %collective-permute-start.8 = (bf16[2,8,256,128]{3,2,1,0:T(8,128)(2,1)}, bf16[2,8,256,128]{3,2,1,0:T(8,128)(2,1)S(1)}, u32[]{:S(2)}, u32[]{:S(2)}) collective-permute-start(bf16[2,8,256,128]{3,2,1,0:T(8,128)(2,1)} %get-tuple-element.31), channel_id=1, source_target_pairs={{8,0},{10,2},{12,4},{14,6},{16,8},{18,10},{20,12},{22,14},{24,16},... | collective-permute-start | bytes 3145736 | tf_op jit(solution)/shard_map/ppermute | solution.py:21
  180.7 21.3 %slice-start = ((s8[5242880]{0:T(1024)(128)(4,1)}), s8[4194304]{0:T(1024)(128)(4,1)S(1)}, s32[]{:S(2)}) async-start(s8[5242880]{0:T(1024)(128)(4,1)} %bitcast.176), calls=%async_computation.3 | async-start | bytes 8388608
  184.3 17.8 %slice-start.1 = ((s8[5242880]{0:T(1024)(128)(4,1)}), s8[1048576]{0:T(1024)(128)(4,1)S(1)}, s32[]{:S(2)}) async-start(s8[5242880]{0:T(1024)(128)(4,1)} %bitcast.176), calls=%async_computation.4 | async-start | bytes 2097152
  255.8 8.8 %copy-start.9 = (f32[8,256,1]{2,1,0:T(8,128)S(1)}, f32[8,256,1]{2,1,0:T(8,128)}, u32[]{:S(2)}) copy-start(f32[8,256,1]{2,1,0:T(8,128)} %get-tuple-element.12) | copy-start | bytes 24580
  266.6 91.1 %collective-permute-start.9 = (f32[8,3,256]{2,1,0:T(4,128)S(1)}, f32[8,3,256]{2,1,0:T(4,128)S(1)}, u32[]{:S(2)}, u32[]{:S(2)}) collective-permute-start(f32[8,3,256]{2,1,0:T(4,128)S(1)} %get-tuple-element.45), channel_id=1, source_target_pairs={{2,0},{4,2},{6,4},{8,6},{10,8},{12,10},{14,12},{16,14},{18,16},{20... | collective-permute-start | bytes 73736 | tf_op jit(solution)/shard_map/ppermute | solution.py:21
  297.0 60.8 %collective-permute-start.10 = (f32[8,3,256]{2,1,0:T(4,128)S(1)}, f32[8,3,256]{2,1,0:T(4,128)S(1)}, u32[]{:S(2)}, u32[]{:S(2)}) collective-permute-start(f32[8,3,256]{2,1,0:T(4,128)S(1)} %get-tuple-element.45), channel_id=1, source_target_pairs={{4,0},{6,2},{8,4},{10,6},{12,8},{14,10},{16,12},{18,14},{20,16},{2... | collective-permute-start | bytes 73736 | tf_op jit(solution)/shard_map/ppermute | solution.py:21
  318.2 39.6 %collective-permute-start.11 = (f32[8,3,256]{2,1,0:T(4,128)S(1)}, f32[8,3,256]{2,1,0:T(4,128)S(1)}, u32[]{:S(2)}, u32[]{:S(2)}) collective-permute-start(f32[8,3,256]{2,1,0:T(4,128)S(1)} %get-tuple-element.45), channel_id=1, source_target_pairs={{6,0},{8,2},{10,4},{12,6},{14,8},{16,10},{18,12},{20,14},{22,16},{... | collective-permute-start | bytes 73736 | tf_op jit(solution)/shard_map/ppermute | solution.py:21
  320.1 37.7 %collective-permute-start.12 = (f32[8,3,256]{2,1,0:T(4,128)S(1)}, f32[8,3,256]{2,1,0:T(4,128)S(1)}, u32[]{:S(2)}, u32[]{:S(2)}) collective-permute-start(f32[8,3,256]{2,1,0:T(4,128)S(1)} %get-tuple-element.45), channel_id=1, source_target_pairs={{8,0},{10,2},{12,4},{14,6},{16,8},{18,10},{20,12},{22,14},{24,16},... | collective-permute-start | bytes 73736 | tf_op jit(solution)/shard_map/ppermute | solution.py:21
  357.9 0.7 copy-start.18
  358.5 25.8 %copy-start.17 = (f32[8,256,128]{2,1,0:T(8,128)S(1)}, f32[8,256,128]{2,1,0:T(8,128)}, u32[]{:S(2)}) copy-start(f32[8,256,128]{2,1,0:T(8,128)} %get-tuple-element.9) | copy-start | bytes 3145732
  390.0 4.5 %copy-start.1 = (bf16[1,512,2048]{2,1,0:T(8,128)(2,1)S(1)}, bf16[1,512,2048]{2,1,0:T(8,128)(2,1)}, u32[]{:S(2)}) copy-start(bf16[1,512,2048]{2,1,0:T(8,128)(2,1)} %param.11) | copy-start | bytes 6291460
Sparse Core Ops, SparseCore 0:
  10.1 34.1 all-gather.3
  62.3 141.0 all-gather.5
  205.5 82.2 all-gather.7
where the time goes:
time: 405 us; the launch traced here: 401 us
  waiting for transfers between devices  139 us (34%)
  starting transfers between devices  76.8 us (19%)
  Pallas kernels  55.3 us (14%)
  local copies, waits for them, and re-layouts  54 us (13%)
  blocking collectives  30.2 us (7%)
  other arithmetic  24.4 us (6%)
  between operations  15.2 us (4%)
  matrix products  5.86 us (1%)
    ppermute x12, waiting for transfers between devices, passed_along(): return lax.ppermute(value, axis, pairs)  104 us
    ppermute x12, starting transfers between devices, passed_along(): return lax.ppermute(value, axis, pairs)  75.9 us
    pallas_call x2, Pallas kernels, run_per_head(): pl.pallas_call(kernel, grid=(heads,), in_specs=[per_head(x.shape) for x i...  55.3 us
    all_gather x1, waiting for transfers between devices, shards(): lax.all_gather(lax.dynamic_slice_in_dim(out_weight, core * half_width, ha...  34.5 us
    all_gather x1, blocking collectives, shards(): lax.all_gather(take_stats(own_stats, par_long), 'seq', axis=2, tiled=True)  30.2 us
    unnamed x72, local copies, waits for them, and re-layouts  15.3 us
  transfers between devices with their start and end apart: 16, of which 6 were waited for; matrix products, arithmetic and copies ran while one was open for 16% of the time, Pallas kernels for 7%

commit v1 on v0

--- a/solution.py
+++ b/solution.py
@@ -270,9 +270,18 @@
         [row_shape, stat_shape, stat_shape, stat_shape],
     )
     own_stats = jnp.stack([top[:, :, 0], inverse[:, :, 0], delta[:, :, 0]], axis=1)
-    near_stats = [own_stats] + [passed_along(own_stats, "seq", -d) for d in near_steps]
-    near_stats = jnp.concatenate(near_stats, axis=2)
-    all_stats_long = lax.all_gather(take_stats(own_stats, par_long), "seq", axis=2, tiled=True)
+    all_stats = lax.all_gather(own_stats, "seq", axis=0, tiled=False)
+    all_stats_long = take_stats(
+        jnp.transpose(all_stats, (1, 2, 0, 3)).reshape(head_count, 3, devices * rows_short),
+        par_long,
+    )
+    spare = jnp.zeros((len(near_steps),) + own_stats.shape, own_stats.dtype)
+    near_stats = lax.dynamic_slice_in_dim(
+        jnp.concatenate([all_stats, spare], axis=0), shard_index, len(near_steps) + 1, axis=0
+    )
+    near_stats = jnp.transpose(near_stats, (1, 2, 0, 3)).reshape(
+        head_count, 3, (len(near_steps) + 1) * rows_short
+    )
 
     query_pos_short = window_positions(
         shard_index, list(range(len(near_steps) + 1)), tok_dev, 2, par_short, rows_short

time: 405 us -> 417 us (1.030)
  starting transfers between devices: 76.8 us -> 22.1 us
  blocking collectives: 30.2 us -> 68.2 us
  local copies, waits for them, and re-layouts: 54 us -> 78.8 us
    ppermute x12 -> x8, starting transfers between devices: 75.9 us -> 21.2 us  [passed_along(): return lax.ppermute(value, axis, pairs)]
    all_gather x1, blocking collectives: 30.2 us -> 68.2 us  [shards(): all_stats = lax.all_gather(own_stats, 'seq', axis=0, tiled=False)]
    unnamed x72 -> x67, local copies, waits for them, and re-layouts: 15.3 us -> 31.7 us
    slice x0 -> x1, local copies, waits for them, and re-layouts: none -> 11 us  [take_stats(): paired[..., 0]]
    pallas_call x3 -> x0, local copies, waits for them, and re-layouts: 7.25 us -> none  [run_per_head(): pl.pallas_call(kernel, grid=(heads,), in_specs=[per_head(x.shape) for x i...]
    ppermute x12 -> x8, waiting for transfers between devices: 104 us -> 104 us  [passed_along(): return lax.ppermute(value, axis, pairs)]
  transfers between devices with their start and end apart: 16 -> 12, of which waited for: 6 -> 6; matrix products, arithmetic and copies ran while one was open for 16% -> 21% of each run, Pallas kernels for 7% -> 7%
where the time goes in v1:
time: 417 us; the launch traced here: 411 us
  waiting for transfers between devices  139 us (33%)
  local copies, waits for them, and re-layouts  78.8 us (19%)
  blocking collectives  68.2 us (16%)
  Pallas kernels  55.3 us (13%)
  other arithmetic  26.3 us (6%)
  starting transfers between devices  22.1 us (5%)
  between operations  15.1 us (4%)
  matrix products  5.86 us (1%)
    ppermute x8, waiting for transfers between devices, passed_along(): return lax.ppermute(value, axis, pairs)  104 us
    all_gather x1, blocking collectives, shards(): all_stats = lax.all_gather(own_stats, 'seq', axis=0, tiled=False)  68.2 us
    pallas_call x2, Pallas kernels, run_per_head(): pl.pallas_call(kernel, grid=(heads,), in_specs=[per_head(x.shape) for x i...  55.3 us
    all_gather x1, waiting for transfers between devices, shards(): lax.all_gather(lax.dynamic_slice_in_dim(out_weight, core * half_width, ha...  34.5 us
    unnamed x67, local copies, waits for them, and re-layouts  31.7 us
    ppermute x8, starting transfers between devices, passed_along(): return lax.ppermute(value, axis, pairs)  21.2 us
    slice x1, local copies, waits for them, and re-layouts, take_stats(): paired[..., 0]  11 us
  transfers between devices with their start and end apart: 12, of which 6 were waited for; matrix products, arithmetic and copies ran while one was open for 21% of the time, Pallas kernels for 7%

profile of v1, /device:TPU:5, one launch (start us, length us, event | category | flops | bytes accessed | tf_op | source)
XLA Modules:
  0.0 410.9 jit_solution(17044673990970199254)
XLA Ops:
  7.3 2.5 constant_dynamic-slice_fusion
  9.8 34.5 %all-gather.5.cloned.1.call-done = bf16[1024,1024]{1,0:T(8,128)(2,1)} async-done(((bf16[512,1024]{1,0:T(8,128)(2,1)}), bf16[1024,1024]{1,0:T(8,128)(2,1)}) %all-gather.5.cloned.1.call-update) | async-done | bytes 2097168 | tf_op jit(solution)/shard_map/all_gather | solution.py:216
  45.1 2.6 copy.169
  52.4 2.9 fusion.4
  55.3 3.0 fusion
  61.0 1.2 fusion.11
  66.5 2.3 bitcast_select_fusion.1
  68.8 1.8 pad_maximum_fusion
  70.6 3.0 collective-permute-start.1
  73.6 3.1 collective-permute-start.2
  76.7 2.7 collective-permute-start.3
  80.7 1.8 convert_select_fusion
  83.2 4.1 collective-permute-start.4
  87.3 1.8 pad_maximum_fusion.2
  89.1 3.0 collective-permute-start.5
  92.2 1.4 copy.118.qss_ref.kss_ref
  94.3 17.0 %collective-permute-done.1 = bf16[2,8,256,128]{3,2,1,0:T(8,128)(2,1)} collective-permute-done((bf16[2,8,256,128]{3,2,1,0:T(8,128)(2,1)}, bf16[2,8,256,128]{3,2,1,0:T(8,128)(2,1)}, u32[]{:S(2)}, u32[]{:S(2)}) %collective-permute-start.1) | collective-permute-done | bytes 1048608 | tf_op jit(solution)/shard_map/ppermute | solution.py:21
  111.3 1.9 collective-permute-start.6
  113.2 64.1 %collective-permute-done.2 = bf16[2,8,256,128]{3,2,1,0:T(8,128)(2,1)} collective-permute-done((bf16[2,8,256,128]{3,2,1,0:T(8,128)(2,1)}, bf16[2,8,256,128]{3,2,1,0:T(8,128)(2,1)}, u32[]{:S(2)}, u32[]{:S(2)}) %collective-permute-start.2) | collective-permute-done | bytes 1048608 | tf_op jit(solution)/shard_map/ppermute | solution.py:21
  177.3 1.9 collective-permute-start.7
  179.3 1.5 collective-permute-start.8
  180.7 3.6 bitcast_select_fusion.2
  184.3 1.5 constant_dynamic-update-slice_fusion.3
  185.8 1.4 constant_dynamic-update-slice_fusion.2
  187.2 1.4 constant_dynamic-update-slice_fusion.1
  188.6 12.0 %collective-permute-done.4 = bf16[2,8,256,128]{3,2,1,0:T(8,128)(2,1)} collective-permute-done((bf16[2,8,256,128]{3,2,1,0:T(8,128)(2,1)}, bf16[2,8,256,128]{3,2,1,0:T(8,128)(2,1)}, u32[]{:S(2)}, u32[]{:S(2)}) %collective-permute-start.4) | collective-permute-done | bytes 1048608 | tf_op jit(solution)/shard_map/ppermute | solution.py:21
  200.5 1.5 constant_dynamic-update-slice_fusion
  202.1 1.4 constant_dynamic-update-slice_fusion.18
  203.6 10.1 %collective-permute-done.7 = bf16[2,8,256,128]{3,2,1,0:T(8,128)(2,1)S(1)} collective-permute-done((bf16[2,8,256,128]{3,2,1,0:T(8,128)(2,1)}, bf16[2,8,256,128]{3,2,1,0:T(8,128)(2,1)S(1)}, u32[]{:S(2)}, u32[]{:S(2)}) %collective-permute-start.7) | collective-permute-done | bytes 1048608 | tf_op jit(solution)/shard_map/ppermute | solution.py:21
  215.0 2.7 slice_bitcast_fusion.6
  217.7 2.8 slice_bitcast_fusion.4
  220.5 5.8 %slice_bitcast_fusion.2 = (bf16[8,2048,128]{2,1,0:T(8,128)(2,1)}, bf16[8,2048,128]{2,1,0:T(8,128)(2,1)}) fusion(bf16[2,8,2048,128]{3,2,1,0:T(8,128)(2,1)} %all-gather.7.cloned.1.call-done), kind=kLoop, calls=%fused_computation.2 | loop fusion | bytes 16777216 | tf_op jit(solution)/shard_map/squeeze | solution.py:261
  226.4 29.4 %shard_map.103 = (f32[8,256,128]{2,1,0:T(8,128)}, f32[8,256,1]{2,1,0:T(8,128)}, f32[8,256,1]{2,1,0:T(8,128)}, f32[8,256,1]{2,1,0:T(8,128)}) custom-call(bf16[8,256,128]{2,1,0:T(8,128)(2,1)} %get-tuple-element.78.q_ref, bf16[8,256,128]{2,1,0:T(8,128)(2,1)} %get-tuple-element.76.g_ref, bf16[8,1280,128]{2,1,0:T(8,128)(2,1)} %get-tuple-element.28.ks_ref, ...), custom_call_target="tpu_custom_call" | custom-call | tf_op jit(solution)/shard_map/pallas_call | solution.py:157
  255.8 1.6 reduce
  257.4 1.6 reduce.1
  259.0 1.6 reduce.2
  260.5 68.2 %all-gather = f32[128,3,256]{2,0,1:T(8,128)S(1)} all-gather(f32[8,3,256]{2,0,1:T(8,128)S(1)} %pad_maximum_fusion.7), channel_id=2, replica_groups=mesh['seq'=16,'fsdp'=2] {'seq'}, dimensions={0}, use_global_device_ids=true | all-gather | bytes 417792 | tf_op jit(solution)/shard_map/all_gather | solution.py:273
  328.7 3.9 copy.135
  332.7 11.0 %fusion.30 = (f32[8,3,2048,1]{0,3,2,1:T(1,128)}, f32[8,3,2048,1]{0,3,2,1:T(1,128)}) fusion(f32[8,3,2048,2]{0,3,2,1:T(2,128)} %bitcast.180), kind=kLoop, calls=%fused_computation.133 | loop fusion | bytes 786432 | tf_op jit(solution)/shard_map/slice | solution.py:40
  343.8 8.6 %copy.167 = f32[8,3,2048,1]{2,1,0,3:T(4,128)S(1)} copy(f32[8,3,2048,1]{0,3,2,1:T(1,128)} %get-tuple-element.23) | data formatting | bytes 393216
  352.3 8.6 %copy.168 = f32[8,3,2048,1]{2,1,0,3:T(4,128)S(1)} copy(f32[8,3,2048,1]{0,3,2,1:T(1,128)} %get-tuple-element.24) | data formatting | bytes 393216
  362.6 5.8 %slice_bitcast_fusion = (bf16[8,2048,128]{2,1,0:T(8,128)(2,1)}, bf16[8,2048,128]{2,1,0:T(8,128)(2,1)}) fusion(bf16[2,8,2048,128]{3,2,1,0:T(8,128)(2,1)} %all-gather.9.cloned.1.call-done), kind=kLoop, calls=%fused_computation | loop fusion | bytes 16777216 | tf_op jit(solution)/shard_map/squeeze | solution.py:300
  368.3 25.8 %shard_map.104 = (f32[8,256,128]{2,1,0:T(8,128)}, f32[8,256,128]{2,1,0:T(8,128)}) custom-call(bf16[8,256,128]{2,1,0:T(8,128)(2,1)} %get-tuple-element.77.k_ref, bf16[8,256,128]{2,1,0:T(8,128)(2,1)} %get-tuple-element.75.v_ref, bf16[8,1280,128]{2,1,0:T(8,128)(2,1)} %get-tuple-element.26.qs_ref, bf16[8,1280,128]{2,1,0:T(8,128)(2,1)} %get-tuple-element.25.gs_ref, ...), custom_call_target="tpu_custom_call" | custom-call | tf_op jit(solution)/shard_map/pallas_call | solution.py:157
  394.2 2.8 select_bitcast_fusion.5
  397.8 1.3 reshape.919
  399.8 1.3 reshape.917
  401.1 1.3 pad_maximum_fusion.1
  403.1 1.3 reshape.914
  (125 shorter events, 19.9 us)
Async XLA Ops:
  7.2 45.2 %copy-start = (bf16[1,512,2048]{2,1,0:T(8,128)(2,1)S(1)}, bf16[1,512,2048]{2,1,0:T(8,128)(2,1)}, u32[]{:S(2)}) copy-start(bf16[1,512,2048]{2,1,0:T(8,128)(2,1)} %param.11) | copy-start | bytes 6291460
  7.2 40.5 %copy-start.14 = (bf16[1,512,1024]{2,1,0:T(8,128)(2,1)S(1)}, bf16[1,512,1024]{2,1,0:T(8,128)(2,1)}, u32[]{:S(2)}) copy-start(bf16[1,512,1024]{2,1,0:T(8,128)(2,1)} %param.9) | copy-start | bytes 3145732
  7.2 37.1 %all-gather.5.cloned.1.call-start = ((), (), s32[]{:S(2)}) async-start(), calls=%async_computation | async-start | bytes 3145728 | tf_op jit(solution)/shard_map/all_gather | solution.py:216
  9.7 210.8 %all-gather.7.cloned.1.call-start = ((), (), s32[]{:S(2)}) async-start(), calls=%async_computation.1 | async-start | bytes 8912896 | tf_op jit(solution)/shard_map/all_gather | solution.py:202
  44.3 11.0 %collective-permute-start = (bf16[1024,1024]{1,0:T(8,128)(2,1)}, bf16[1024,1024]{1,0:T(8,128)(2,1)}, u32[]{:S(2)}, u32[]{:S(2)}) collective-permute-start(bf16[1024,1024]{1,0:T(8,128)(2,1)} %all-gather.5.cloned.1.call-done), channel_id=1, source_target_pairs={{0,2},{2,0},{4,6},{6,4},{8,10},{10,8},{12,14},{14,12},{16,18},{18,... | collective-permute-start | bytes 6291464 | tf_op jit(solution)/shard_map/ppermute | solution.py:222
  45.1 2.8 copy-start.15
  48.2 4.1 %copy-start.17 = (s32[8]{0:T(128)S(1)}, s32[8]{0:T(128)}, u32[]{:S(2)}) copy-start(s32[8]{0:T(128)} %param.13) | copy-start | bytes 100
  48.6 1.9 copy-start.4
  48.6 2.8 copy-start.2
  55.3 3.3 copy-start.9
  58.6 1.4 copy-start.10
  58.6 1.4 copy-start.11
  58.6 1.5 copy-start.12
  58.6 1.9 copy-start.13
  59.0 0.8 copy-start.6
  59.0 1.0 copy-start.7
  60.5 2.6 copy-start.18
  60.5 6.0 %copy-start.3 = (bf16[8,256,1,128]{3,0,2,1:T(8,128)(2,1)S(1)}, bf16[8,256,1,128]{3,0,2,1:T(8,128)(2,1)}, u32[]{:S(2)}) copy-start(bf16[8,256,1,128]{3,0,2,1:T(8,128)(2,1)} %copy-done.2) | copy-start | bytes 1572868
  60.5 6.0 %copy-start.5 = (bf16[8,256,1,128]{3,0,2,1:T(8,128)(2,1)S(1)}, bf16[8,256,1,128]{3,0,2,1:T(8,128)(2,1)}, u32[]{:S(2)}) copy-start(bf16[8,256,1,128]{3,0,2,1:T(8,128)(2,1)} %copy-done.4) | copy-start | bytes 1572868
  62.2 300.4 %all-gather.9.cloned.1.call-start = ((), (), s32[]{:S(2)}) async-start(), calls=%async_computation.2 | async-start | bytes 8912896 | tf_op jit(solution)/shard_map/all_gather | solution.py:202
  70.6 40.7 %collective-permute-start.1 = (bf16[2,8,256,128]{3,2,1,0:T(8,128)(2,1)}, bf16[2,8,256,128]{3,2,1,0:T(8,128)(2,1)}, u32[]{:S(2)}, u32[]{:S(2)}) collective-permute-start(bf16[2,8,256,128]{3,2,1,0:T(8,128)(2,1)} %get-tuple-element.37), channel_id=1, source_target_pairs={{0,2},{2,4},{4,6},{6,8},{8,10},{10,12},{12,14},{14,16},{16,18},{18... | collective-permute-start | bytes 3145736 | tf_op jit(solution)/shard_map/ppermute | solution.py:21
  73.6 103.8 %collective-permute-start.2 = (bf16[2,8,256,128]{3,2,1,0:T(8,128)(2,1)}, bf16[2,8,256,128]{3,2,1,0:T(8,128)(2,1)}, u32[]{:S(2)}, u32[]{:S(2)}) collective-permute-start(bf16[2,8,256,128]{3,2,1,0:T(8,128)(2,1)} %get-tuple-element.37), channel_id=1, source_target_pairs={{0,4},{2,6},{4,8},{6,10},{8,12},{10,14},{12,16},{14,18},{16,20},{1... | collective-permute-start | bytes 3145736 | tf_op jit(solution)/shard_map/ppermute | solution.py:21
  76.7 102.6 %collective-permute-start.3 = (bf16[2,8,256,128]{3,2,1,0:T(8,128)(2,1)}, bf16[2,8,256,128]{3,2,1,0:T(8,128)(2,1)}, u32[]{:S(2)}, u32[]{:S(2)}) collective-permute-start(bf16[2,8,256,128]{3,2,1,0:T(8,128)(2,1)} %get-tuple-element.37), channel_id=1, source_target_pairs={{0,6},{2,8},{4,10},{6,12},{8,14},{10,16},{12,18},{14,20},{16,22},{... | collective-permute-start | bytes 3145736 | tf_op jit(solution)/shard_map/ppermute | solution.py:21
  83.2 117.3 %collective-permute-start.4 = (bf16[2,8,256,128]{3,2,1,0:T(8,128)(2,1)}, bf16[2,8,256,128]{3,2,1,0:T(8,128)(2,1)}, u32[]{:S(2)}, u32[]{:S(2)}) collective-permute-start(bf16[2,8,256,128]{3,2,1,0:T(8,128)(2,1)} %get-tuple-element.37), channel_id=1, source_target_pairs={{0,8},{2,10},{4,12},{6,14},{8,16},{10,18},{12,20},{14,22},{16,24},... | collective-permute-start | bytes 3145736 | tf_op jit(solution)/shard_map/ppermute | solution.py:21
  89.1 112.9 %collective-permute-start.5 = (bf16[2,8,256,128]{3,2,1,0:T(8,128)(2,1)}, bf16[2,8,256,128]{3,2,1,0:T(8,128)(2,1)}, u32[]{:S(2)}, u32[]{:S(2)}) collective-permute-start(bf16[2,8,256,128]{3,2,1,0:T(8,128)(2,1)} %get-tuple-element.33), channel_id=1, source_target_pairs={{2,0},{4,2},{6,4},{8,6},{10,8},{12,10},{14,12},{16,14},{18,16},{20... | collective-permute-start | bytes 3145736 | tf_op jit(solution)/shard_map/ppermute | solution.py:21
  93.6 90.7 %copy-start.8 = (bf16[2,8,1280,128]{3,2,1,0:T(8,128)(2,1)S(1)}, bf16[2,8,1280,128]{3,2,1,0:T(8,128)(2,1)}, u32[]{:S(2)}) copy-start(bf16[2,8,1280,128]{3,2,1,0:T(8,128)(2,1)} %get-tuple-element.38) | copy-start | bytes 15728644
  111.3 92.2 %collective-permute-start.6 = (bf16[2,8,256,128]{3,2,1,0:T(8,128)(2,1)}, bf16[2,8,256,128]{3,2,1,0:T(8,128)(2,1)S(1)}, u32[]{:S(2)}, u32[]{:S(2)}) collective-permute-start(bf16[2,8,256,128]{3,2,1,0:T(8,128)(2,1)} %get-tuple-element.33), channel_id=1, source_target_pairs={{4,0},{6,2},{8,4},{10,6},{12,8},{14,10},{16,12},{18,14},{20,16},{2... | collective-permute-start | bytes 3145736 | tf_op jit(solution)/shard_map/ppermute | solution.py:21
  177.3 36.4 %collective-permute-start.7 = (bf16[2,8,256,128]{3,2,1,0:T(8,128)(2,1)}, bf16[2,8,256,128]{3,2,1,0:T(8,128)(2,1)S(1)}, u32[]{:S(2)}, u32[]{:S(2)}) collective-permute-start(bf16[2,8,256,128]{3,2,1,0:T(8,128)(2,1)} %get-tuple-element.33), channel_id=1, source_target_pairs={{6,0},{8,2},{10,4},{12,6},{14,8},{16,10},{18,12},{20,14},{22,16},{... | collective-permute-start | bytes 3145736 | tf_op jit(solution)/shard_map/ppermute | solution.py:21
  179.3 35.6 %collective-permute-start.8 = (bf16[2,8,256,128]{3,2,1,0:T(8,128)(2,1)}, bf16[2,8,256,128]{3,2,1,0:T(8,128)(2,1)S(1)}, u32[]{:S(2)}, u32[]{:S(2)}) collective-permute-start(bf16[2,8,256,128]{3,2,1,0:T(8,128)(2,1)} %get-tuple-element.33), channel_id=1, source_target_pairs={{8,0},{10,2},{12,4},{14,6},{16,8},{18,10},{20,12},{22,14},{24,16},... | collective-permute-start | bytes 3145736 | tf_op jit(solution)/shard_map/ppermute | solution.py:21
  180.7 21.3 %slice-start = ((s8[5242880]{0:T(1024)(128)(4,1)}), s8[4194304]{0:T(1024)(128)(4,1)S(1)}, s32[]{:S(2)}) async-start(s8[5242880]{0:T(1024)(128)(4,1)} %bitcast.181), calls=%async_computation.3 | async-start | bytes 8388608
  184.3 17.8 %slice-start.1 = ((s8[5242880]{0:T(1024)(128)(4,1)}), s8[1048576]{0:T(1024)(128)(4,1)S(1)}, s32[]{:S(2)}) async-start(s8[5242880]{0:T(1024)(128)(4,1)} %bitcast.181), calls=%async_computation.4 | async-start | bytes 2097152
  368.3 25.8 %copy-start.16 = (f32[8,256,128]{2,1,0:T(8,128)S(1)}, f32[8,256,128]{2,1,0:T(8,128)}, u32[]{:S(2)}) copy-start(f32[8,256,128]{2,1,0:T(8,128)} %get-tuple-element.9) | copy-start | bytes 3145732
  399.8 4.5 %copy-start.1 = (bf16[1,512,2048]{2,1,0:T(8,128)(2,1)S(1)}, bf16[1,512,2048]{2,1,0:T(8,128)(2,1)}, u32[]{:S(2)}) copy-start(bf16[1,512,2048]{2,1,0:T(8,128)(2,1)} %param.11) | copy-start | bytes 6291460
Sparse Core Ops, SparseCore 0:
  10.1 34.1 all-gather.4
  62.3 141.0 all-gather.6
  205.6 82.1 all-gather.8

commit v2 on v0

--- a/solution.py
+++ b/solution.py
@@ -40,6 +40,39 @@
     return jnp.where((parity == 0)[:, None, None], paired[..., 0], paired[..., 1])
 
 
+def pick_last(tensor, parity):
+    paired = tensor.reshape(tensor.shape[:-1] + (tensor.shape[-1] // 2, 2))
+    cond = (parity == 0).reshape((-1,) + (1,) * (tensor.ndim - 1))
+    return jnp.where(cond, paired[..., 0], paired[..., 1])
+
+
+def put_last(tensor, parity):
+    cond = (parity == 0).reshape((-1,) + (1,) * (tensor.ndim - 1))
+    zero_fill = jnp.zeros_like(tensor)
+    stacked = jnp.stack(
+        [jnp.where(cond, tensor, zero_fill), jnp.where(cond, zero_fill, tensor)], axis=-1
+    )
+    return stacked.reshape(tensor.shape[:-1] + (2 * tensor.shape[-1],))
+
+
+def order_rows(tensor, parity):
+    return jnp.concatenate([take_rows(tensor, parity), take_rows(tensor, 1 - parity)], axis=-2)
+
+
+def unorder_rows(tensor, parity):
+    half = tensor.shape[-2] // 2
+    return put_rows(tensor[..., :half, :], parity) + put_rows(tensor[..., half:, :], 1 - parity)
+
+
+def order_last(tensor, parity):
+    return jnp.concatenate([pick_last(tensor, parity), pick_last(tensor, 1 - parity)], axis=-1)
+
+
+def unorder_last(tensor, parity):
+    half = tensor.shape[-1] // 2
+    return put_last(tensor[..., :half], parity) + put_last(tensor[..., half:], 1 - parity)
+
+
 def segment_of(positions, lengths):
     seg_ends = jnp.cumsum(lengths)
     return jnp.sum((positions[..., None] >= seg_ends).astype(jnp.int32), axis=-1)
@@ -72,33 +105,22 @@
     )
 
 
-def query_kernel(
-    q_ref, g_ref, ks_ref, vs_ref, kl_ref, vl_ref,
-    qpos_ref, qss_ref, qsl_ref, kps_ref, kss_ref, kpl_ref, ksl_ref,
-    dq_ref, top_ref, inv_ref, delta_ref, *, scale,
-):
-    q = q_ref[0]
-    g = g_ref[0]
-    qpos = qpos_ref[0]
-    parts = []
-    for k_ref, v_ref, kp_ref, kseg_ref, qseg_ref in (
-        (ks_ref, vs_ref, kps_ref, kss_ref, qss_ref),
-        (kl_ref, vl_ref, kpl_ref, ksl_ref, qsl_ref),
-    ):
-        k = k_ref[0]
-        live = (kp_ref[0] <= qpos) & (kseg_ref[0] == qseg_ref[0])
-        scores = jnp.where(live, dot_nt(q, k) * scale, VERY_NEGATIVE)
-        parts.append((live, scores, k, v_ref))
-    top = jnp.maximum(
-        jnp.max(parts[0][1], axis=1, keepdims=True), jnp.max(parts[1][1], axis=1, keepdims=True)
-    )
+def attend_rows(q, g, parts, scale):
+    scored = [
+        (k, v, live, jnp.where(live, dot_nt(q, k) * scale, VERY_NEGATIVE))
+        for k, v, live in parts
+    ]
+    top = None
+    for k, v, live, scores in scored:
+        part_top = jnp.max(scores, axis=1, keepdims=True)
+        top = part_top if top is None else jnp.maximum(top, part_top)
     total = None
     numer = None
     weights = []
-    for live, scores, k, v_ref in parts:
+    for k, v, live, scores in scored:
         w = jnp.where(live, jnp.exp(scores - top), 0.0)
         part_total = jnp.sum(w, axis=1, keepdims=True)
-        part_numer = dot_nn(w.astype(jnp.bfloat16), v_ref[0])
+        part_numer = dot_nn(w.astype(jnp.bfloat16), v)
         total = part_total if total is None else total + part_total
         numer = part_numer if numer is None else numer + part_numer
         weights.append(w)
@@ -106,37 +128,44 @@
     delta = jnp.sum(g.astype(jnp.float32) * attended, axis=1, keepdims=True)
     inverse = 1.0 / total
     grad_query = None
-    for (live, scores, k, v_ref), w in zip(parts, weights):
+    for (k, v, live, scores), w in zip(scored, weights):
         probability = w * inverse
-        grad_probs = dot_nt(g, v_ref[0])
+        grad_probs = dot_nt(g, v)
         grad_scores = (probability * (grad_probs - delta)).astype(jnp.bfloat16)
         part = dot_nn(grad_scores, k) * scale
         grad_query = part if grad_query is None else grad_query + part
-    dq_ref[0] = grad_query
-    top_ref[0] = top
-    inv_ref[0] = inverse
-    delta_ref[0] = delta
-
-
-def key_kernel(
-    k_ref, v_ref, qs_ref, gs_ref, ql_ref, gl_ref,
-    kpos_ref, kss_ref, ksl_ref, qps_ref, qss_ref, sts_ref, qpl_ref, qsl_ref, stl_ref,
-    dk_ref, dv_ref, *, scale,
+    return grad_query, top, inverse, delta
+
+
+def query_kernel(
+    q_ref, g_ref, ks_ref, vs_ref, kl_ref, vl_ref,
+    qpos_ref, qss_ref, qsl_ref, kps_ref, kss_ref, kpl_ref, ksl_ref,
+    dq_ref, top_ref, inv_ref, delta_ref, *, scale,
 ):
-    k = k_ref[0]
-    v = v_ref[0]
-    kpos = kpos_ref[0]
+    half = q_ref.shape[1] // 2
+    ks = ks_ref[0]
+    vs = vs_ref[0]
+    for lo, hi, with_long in ((0, half, True), (half, 2 * half, False)):
+        q = q_ref[0, lo:hi, :]
+        g = g_ref[0, lo:hi, :]
+        qpos = qpos_ref[0, lo:hi, :]
+        parts = [(ks, vs, (kps_ref[0] <= qpos) & (kss_ref[0] == qss_ref[0, lo:hi, :]))]
+        if with_long:
+            parts.append(
+                (kl_ref[0], vl_ref[0], (kpl_ref[0] <= qpos) & (ksl_ref[0] == qsl_ref[0, lo:hi, :]))
+            )
+        grad_query, top, inverse, delta = attend_rows(q, g, parts, scale)
+        dq_ref[0, lo:hi, :] = grad_query
+        top_ref[0, lo:hi, :] = top
+        inv_ref[0, lo:hi, :] = inverse
+        delta_ref[0, lo:hi, :] = delta
+
+
+def key_rows(k, v, parts, scale):
     grad_key = None
     grad_value = None
-    for q_ref, g_ref, qp_ref, qseg_ref, kseg_ref, st_ref in (
-        (qs_ref, gs_ref, qps_ref, qss_ref, kss_ref, sts_ref),
-        (ql_ref, gl_ref, qpl_ref, qsl_ref, ksl_ref, stl_ref),
-    ):
-        q = q_ref[0]
-        g = g_ref[0]
-        live = (kpos <= qp_ref[0]) & (kseg_ref[0] == qseg_ref[0])
+    for q, g, live, stats in parts:
         scores = jnp.where(live, dot_nt(k, q) * scale, VERY_NEGATIVE)
-        stats = st_ref[0]
         probability = jnp.where(live, jnp.exp(scores - stats[0:1, :]), 0.0) * stats[1:2, :]
         grad_probs = dot_nt(v, g)
         grad_scores = (probability * (grad_probs - stats[2:3, :])).astype(jnp.bfloat16)
@@ -144,8 +173,35 @@
         part_value = dot_nn(probability.astype(jnp.bfloat16), g)
         grad_key = part_key if grad_key is None else grad_key + part_key
         grad_value = part_value if grad_value is None else grad_value + part_value
-    dk_ref[0] = grad_key
-    dv_ref[0] = grad_value
+    return grad_key, grad_value
+
+
+def key_kernel(
+    k_ref, v_ref, qs_ref, gs_ref, ql_ref, gl_ref,
+    kpos_ref, kss_ref, ksl_ref, qps_ref, qss_ref, sts_ref, qpl_ref, qsl_ref, stl_ref,
+    dk_ref, dv_ref, *, scale,
+):
+    half = k_ref.shape[1] // 2
+    qs = qs_ref[0]
+    gs = gs_ref[0]
+    sts = sts_ref[0]
+    for lo, hi, with_long in ((0, half, True), (half, 2 * half, False)):
+        k = k_ref[0, lo:hi, :]
+        v = v_ref[0, lo:hi, :]
+        kpos = kpos_ref[0, lo:hi, :]
+        parts = [(qs, gs, (kpos <= qps_ref[0]) & (kss_ref[0, lo:hi, :] == qss_ref[0]), sts)]
+        if with_long:
+            parts.append(
+                (
+                    ql_ref[0],
+                    gl_ref[0],
+                    (kpos <= qpl_ref[0]) & (ksl_ref[0, lo:hi, :] == qsl_ref[0]),
+                    stl_ref[0],
+                )
+            )
+        grad_key, grad_value = key_rows(k, v, parts, scale)
+        dk_ref[0, lo:hi, :] = grad_key
+        dv_ref[0, lo:hi, :] = grad_value
 
 
 def per_head(shape):
@@ -253,15 +309,15 @@
     grad_query, top, inverse, delta = run_per_head(
         functools.partial(query_kernel, scale=scale),
         [
-            q_rows,
-            g_rows,
+            order_rows(q_rows, par_long),
+            order_rows(g_rows, par_long),
             near_kv[0],
             near_kv[1],
             all_kv_long[0],
             all_kv_long[1],
-            column(own_pos),
-            column(own_seg_short),
-            column(own_seg_long),
+            column(order_last(own_pos, par_long)),
+            column(order_last(own_seg_short, par_long)),
+            column(order_last(own_seg_long, par_long)),
             row(key_pos_short),
             row(key_seg_short),
             row(long_pos),
@@ -269,7 +325,10 @@
         ],
         [row_shape, stat_shape, stat_shape, stat_shape],
     )
-    own_stats = jnp.stack([top[:, :, 0], inverse[:, :, 0], delta[:, :, 0]], axis=1)
+    grad_query = unorder_rows(grad_query, par_long)
+    own_stats = unorder_last(
+        jnp.stack([top[:, :, 0], inverse[:, :, 0], delta[:, :, 0]], axis=1), par_long
+    )
     near_stats = [own_stats] + [passed_along(own_stats, "seq", -d) for d in near_steps]
     near_stats = jnp.concatenate(near_stats, axis=2)
     all_stats_long = lax.all_gather(take_stats(own_stats, par_long), "seq", axis=2, tiled=True)
@@ -283,15 +342,15 @@
     grad_key, grad_value = run_per_head(
         functools.partial(key_kernel, scale=scale),
         [
-            own_kv[0],
-            own_kv[1],
+            order_rows(own_kv[0], par_long),
+            order_rows(own_kv[1], par_long),
             near_qg[0],
             near_qg[1],
             all_qg_long[0],
             all_qg_long[1],
-            column(own_pos),
-            column(own_seg_short),
-            column(own_seg_long),
+            column(order_last(own_pos, par_long)),
+            column(order_last(own_seg_short, par_long)),
+            column(order_last(own_seg_long, par_long)),
             row(query_pos_short),
             row(query_seg_short),
             near_stats,
@@ -301,6 +360,8 @@
         ],
         [row_shape, row_shape],
     )
+    grad_key = unorder_rows(grad_key, par_long)
+    grad_value = unorder_rows(grad_value, par_long)
 
     def to_tokens(rows_here):
         tokens = put_rows(rows_here.astype(jnp.bfloat16), par_short)

time: 405 us -> 375 us (0.926)
  starting transfers between devices: 76.8 us -> 63 us
  Pallas kernels: 55.3 us -> 44 us
  local copies, waits for them, and re-layouts: 54 us -> 45.4 us
  blocking collectives: 30.2 us -> 22.4 us
  waiting for transfers between devices: 139 us -> 145 us
  other arithmetic: 24.4 us -> 29.8 us
    ppermute x12, starting transfers between devices: 75.9 us -> 62 us  [passed_along(): return lax.ppermute(value, axis, pairs)]
    pallas_call x2, Pallas kernels: 55.3 us -> 44 us  [run_per_head(): pl.pallas_call(kernel, grid=(heads,), in_specs=[per_head(x.shape) for x i...]
    all_gather x1, blocking collectives: 30.2 us -> 22.4 us  [shards(): lax.all_gather(take_stats(own_stats, par_long), 'seq', axis=2, tiled=True)]
    pallas_call x3 -> x0, local copies, waits for them, and re-layouts: 7.25 us -> none  [run_per_head(): pl.pallas_call(kernel, grid=(heads,), in_specs=[per_head(x.shape) for x i...]
    ppermute x12, waiting for transfers between devices: 104 us -> 109 us  [passed_along(): return lax.ppermute(value, axis, pairs)]
    unnamed x72 -> x77, local copies, waits for them, and re-layouts: 15.3 us -> 10.6 us
    select_n x4 -> x5, other arithmetic: 7.51 us -> 8.25 us  [take_rows(): jnp.where((parity == 0)[:, None, None], paired[..., 0, :], paired[..., 1,...]
  transfers between devices with their start and end apart: 16 -> 16, of which waited for: 6 -> 7; matrix products, arithmetic and copies ran while one was open for 16% -> 15% of each run, Pallas kernels for 7% -> 7%
where the time goes in v2:
time: 375 us; the launch traced here: 370 us
  waiting for transfers between devices  145 us (39%)
  starting transfers between devices  63 us (17%)
  local copies, waits for them, and re-layouts  45.4 us (12%)
  Pallas kernels  44 us (12%)
  other arithmetic  29.8 us (8%)
  blocking collectives  22.4 us (6%)
  between operations  15.3 us (4%)
  matrix products  5.86 us (2%)
    ppermute x12, waiting for transfers between devices, passed_along(): return lax.ppermute(value, axis, pairs)  109 us
    ppermute x12, starting transfers between devices, passed_along(): return lax.ppermute(value, axis, pairs)  62 us
    pallas_call x2, Pallas kernels, run_per_head(): pl.pallas_call(kernel, grid=(heads,), in_specs=[per_head(x.shape) for x i...  44 us
    all_gather x1, waiting for transfers between devices, shards(): lax.all_gather(lax.dynamic_slice_in_dim(out_weight, core * half_width, ha...  34.5 us
    all_gather x1, blocking collectives, shards(): lax.all_gather(take_stats(own_stats, par_long), 'seq', axis=2, tiled=True)  22.4 us
    unnamed x77, local copies, waits for them, and re-layouts  10.6 us
    select_n x5, other arithmetic, take_rows(): jnp.where((parity == 0)[:, None, None], paired[..., 0, :], paired[..., 1,...  8.25 us
  transfers between devices with their start and end apart: 16, of which 7 were waited for; matrix products, arithmetic and copies ran while one was open for 15% of the time, Pallas kernels for 7%

profile of v2, /device:TPU:5, one launch (start us, length us, event | category | flops | bytes accessed | tf_op | source)
XLA Modules:
  0.0 370.4 jit_solution(12805672270738671204)
XLA Ops:
  7.3 2.5 constant_dynamic-slice_fusion
  9.8 34.5 %all-gather.4.cloned.1.call-done = bf16[1024,1024]{1,0:T(8,128)(2,1)} async-done(((bf16[512,1024]{1,0:T(8,128)(2,1)}), bf16[1024,1024]{1,0:T(8,128)(2,1)}) %all-gather.4.cloned.1.call-update) | async-done | bytes 2097168 | tf_op jit(solution)/shard_map/all_gather | solution.py:272
  45.1 2.6 copy.362
  51.6 2.9 fusion.5
  54.5 3.0 fusion
  60.0 1.2 fusion.11
  63.5 1.4 copy.296.qpos_ref.kpos_ref
  64.9 1.3 copy.297.qss_ref.kss_ref
  69.6 4.5 %bitcast_select_fusion.5 = (bf16[1,8,256,128]{3,2,1,0:T(8,128)(2,1)}, bf16[1,8,256,128]{3,2,1,0:T(8,128)(2,1)S(1)}, bf16[1,8,256,128]{3,2,1,0:T(8,128)(2,1)}, bf16[1,8,256,128]{3,2,1,0:T(8,128)(2,1)S(1)}) fusion(pred[8]{0:T(512)(128)(4,1)S(1)} %get-tuple-element.136, bf16[8,256,1,128]{3,0,2,1:T(8,128)(2,1)} %copy-done.12, ...), kind=kLoop, calls=%fused_computation.51 | loop fusion | flops 1048576 | bytes 6291464 | tf_op jit(solution)/shard_map/jit(_where)/select_n | solution.py:27
  74.0 1.8 pad_maximum_fusion
  75.8 3.0 collective-permute-start.1
  78.9 1.4 copy.298.qsl_ref.ksl_ref
  82.2 3.1 collective-permute-start.2
  85.3 2.7 collective-permute-start.3
  88.0 3.2 collective-permute-start.4
  91.1 1.7 pad_maximum_fusion.2
  92.8 3.0 collective-permute-start.5
  95.9 1.8 copy_select_fusion.4
  98.8 16.8 %collective-permute-done.1 = bf16[2,8,256,128]{3,2,1,0:T(8,128)(2,1)} collective-permute-done((bf16[2,8,256,128]{3,2,1,0:T(8,128)(2,1)}, bf16[2,8,256,128]{3,2,1,0:T(8,128)(2,1)}, u32[]{:S(2)}, u32[]{:S(2)}) %collective-permute-start.1) | collective-permute-done | bytes 1048608 | tf_op jit(solution)/shard_map/ppermute | solution.py:21
  115.6 1.9 collective-permute-start.6
  118.4 54.9 %collective-permute-done.2 = bf16[2,8,256,128]{3,2,1,0:T(8,128)(2,1)S(1)} collective-permute-done((bf16[2,8,256,128]{3,2,1,0:T(8,128)(2,1)}, bf16[2,8,256,128]{3,2,1,0:T(8,128)(2,1)S(1)}, u32[]{:S(2)}, u32[]{:S(2)}) %collective-permute-start.2) | collective-permute-done | bytes 1048608 | tf_op jit(solution)/shard_map/ppermute | solution.py:21
  173.2 1.9 collective-permute-start.7
  176.0 6.2 %collective-permute-done.3 = bf16[2,8,256,128]{3,2,1,0:T(8,128)(2,1)S(1)} collective-permute-done((bf16[2,8,256,128]{3,2,1,0:T(8,128)(2,1)}, bf16[2,8,256,128]{3,2,1,0:T(8,128)(2,1)S(1)}, u32[]{:S(2)}, u32[]{:S(2)}) %collective-permute-start.3) | collective-permute-done | bytes 1048608 | tf_op jit(solution)/shard_map/ppermute | solution.py:21
  182.2 1.5 collective-permute-start.8
  184.5 1.4 constant_dynamic-update-slice_fusion.3
  186.1 13.5 %collective-permute-done.4 = bf16[2,8,256,128]{3,2,1,0:T(8,128)(2,1)S(1)} collective-permute-done((bf16[2,8,256,128]{3,2,1,0:T(8,128)(2,1)}, bf16[2,8,256,128]{3,2,1,0:T(8,128)(2,1)S(1)}, u32[]{:S(2)}, u32[]{:S(2)}) %collective-permute-start.4) | collective-permute-done | bytes 1048608 | tf_op jit(solution)/shard_map/ppermute | solution.py:21
  200.1 10.1 %collective-permute-done.7 = bf16[2,8,256,128]{3,2,1,0:T(8,128)(2,1)S(1)} collective-permute-done((bf16[2,8,256,128]{3,2,1,0:T(8,128)(2,1)S(1)}, bf16[2,8,256,128]{3,2,1,0:T(8,128)(2,1)S(1)}, u32[]{:S(2)}, u32[]{:S(2)}) %collective-permute-start.7) | collective-permute-done | bytes 1048608 | tf_op jit(solution)/shard_map/ppermute | solution.py:21
  210.4 7.9 %collective-permute-done.8 = bf16[2,8,256,128]{3,2,1,0:T(8,128)(2,1)S(1)} collective-permute-done((bf16[2,8,256,128]{3,2,1,0:T(8,128)(2,1)S(1)}, bf16[2,8,256,128]{3,2,1,0:T(8,128)(2,1)S(1)}, u32[]{:S(2)}, u32[]{:S(2)}) %collective-permute-start.8) | collective-permute-done | bytes 1048608 | tf_op jit(solution)/shard_map/ppermute | solution.py:21
  218.5 2.7 slice_bitcast_fusion.6
  221.3 2.8 slice_bitcast_fusion.4
  224.1 5.9 %slice_bitcast_fusion.2 = (bf16[8,2048,128]{2,1,0:T(8,128)(2,1)}, bf16[8,2048,128]{2,1,0:T(8,128)(2,1)}) fusion(bf16[2,8,2048,128]{3,2,1,0:T(8,128)(2,1)} %all-gather.6.cloned.1.call-done), kind=kLoop, calls=%fused_computation.2 | loop fusion | bytes 16777216 | tf_op jit(solution)/shard_map/squeeze | solution.py:317
  229.9 24.6 %shard_map.103 = (f32[8,256,128]{2,1,0:T(8,128)}, f32[8,256,1]{2,1,0:T(8,128)}, f32[8,256,1]{2,1,0:T(8,128)}, f32[8,256,1]{2,1,0:T(8,128)}) custom-call(bf16[8,256,128]{2,1,0:T(8,128)(2,1)} %pad_maximum_fusion.7.q_ref, bf16[8,256,128]{2,1,0:T(8,128)(2,1)} %pad_maximum_fusion.8.g_ref, bf16[8,1280,128]{2,1,0:T(8,128)(2,1)} %get-tuple-element.28.ks_ref, ...), custom_call_target="tpu_custom_call" | custom-call | tf_op jit(solution)/shard_map/pallas_call | solution.py:213
  254.5 1.6 reduce
  256.1 1.6 reduce.1
  257.7 1.6 reduce.2
  259.8 25.9 %collective-permute-start.9 = (f32[8,3,256]{2,1,0:T(4,128)S(1)}, f32[8,3,256]{2,1,0:T(4,128)S(1)}, u32[]{:S(2)}, u32[]{:S(2)}) collective-permute-start(f32[8,3,256]{2,1,0:T(4,128)S(1)} %copy.327), channel_id=1, source_target_pairs={{2,0},{4,2},{6,4},{8,6},{10,8},{12,10},{14,12},{16,14},{18,16},{20... | collective-permute-start | bytes 73736 | tf_op jit(solution)/shard_map/ppermute | solution.py:21
  285.7 12.7 %collective-permute-start.10 = (f32[8,3,256]{2,1,0:T(4,128)S(1)}, f32[8,3,256]{2,1,0:T(4,128)S(1)}, u32[]{:S(2)}, u32[]{:S(2)}) collective-permute-start(f32[8,3,256]{2,1,0:T(4,128)S(1)} %copy.327), channel_id=1, source_target_pairs={{4,0},{6,2},{8,4},{10,6},{12,8},{14,10},{16,12},{18,14},{20,16},{2... | collective-permute-start | bytes 73736 | tf_op jit(solution)/shard_map/ppermute | solution.py:21
  298.4 1.9 collective-permute-start.11
  300.3 1.3 collective-permute-start.12
  301.7 5.8 %slice_bitcast_fusion = (bf16[8,2048,128]{2,1,0:T(8,128)(2,1)}, bf16[8,2048,128]{2,1,0:T(8,128)(2,1)}) fusion(bf16[2,8,2048,128]{3,2,1,0:T(8,128)(2,1)} %all-gather.8.cloned.1.call-done), kind=kLoop, calls=%fused_computation | loop fusion | bytes 16777216 | tf_op jit(solution)/shard_map/squeeze | solution.py:350
  307.5 22.4 %all_gather.15.stl_ref = f32[8,3,2048]{2,1,0:T(4,128)} all-gather(f32[8,3,128]{2,1,0:T(4,128)S(1)} %fusion.17), channel_id=1, replica_groups=mesh['seq'=16,'fsdp'=2] {'seq'}, dimensions={2}, use_global_device_ids=true | all-gather | bytes 208896 | tf_op jit(solution)/shard_map/all_gather | solution.py:334
  330.7 19.4 %shard_map.104 = (f32[8,256,128]{2,1,0:T(8,128)}, f32[8,256,128]{2,1,0:T(8,128)}) custom-call(bf16[8,256,128]{2,1,0:T(8,128)(2,1)} %pad_maximum_fusion.9.k_ref, bf16[8,256,128]{2,1,0:T(8,128)(2,1)} %pad_maximum_fusion.10.v_ref, bf16[8,1280,128]{2,1,0:T(8,128)(2,1)} %get-tuple-element.26.qs_ref, bf16[8,1280,128]{2,1,0:T(8,128)(2,1)} %get-tuple-element.25.gs_ref, ...), custom_call_target="tpu_custom_call" | custom-call | tf_op jit(solution)/shard_map/pallas_call | solution.py:213
  350.1 2.9 select_bitcast_fusion.9
  354.5 1.5 bitcast_select_fusion.7
  356.3 1.3 reshape.970
  357.8 1.3 reshape.968
  359.1 1.3 pad_maximum_fusion.1
  361.6 2.3 reshape.966
  (166 shorter events, 23.0 us)
Async XLA Ops:
  7.2 44.4 %copy-start = (bf16[1,512,2048]{2,1,0:T(8,128)(2,1)S(1)}, bf16[1,512,2048]{2,1,0:T(8,128)(2,1)}, u32[]{:S(2)}) copy-start(bf16[1,512,2048]{2,1,0:T(8,128)(2,1)} %param.11) | copy-start | bytes 6291460
  7.2 40.5 %copy-start.17 = (bf16[1,512,1024]{2,1,0:T(8,128)(2,1)S(1)}, bf16[1,512,1024]{2,1,0:T(8,128)(2,1)}, u32[]{:S(2)}) copy-start(bf16[1,512,1024]{2,1,0:T(8,128)(2,1)} %param.9) | copy-start | bytes 3145732
  7.2 37.1 %all-gather.4.cloned.1.call-start = ((), (), s32[]{:S(2)}) async-start(), calls=%async_computation | async-start | bytes 3145728 | tf_op jit(solution)/shard_map/all_gather | solution.py:272
  9.7 214.3 %all-gather.6.cloned.1.call-start = ((), (), s32[]{:S(2)}) async-start(), calls=%async_computation.1 | async-start | bytes 8912896 | tf_op jit(solution)/shard_map/all_gather | solution.py:258
  44.3 10.2 %collective-permute-start = (bf16[1024,1024]{1,0:T(8,128)(2,1)}, bf16[1024,1024]{1,0:T(8,128)(2,1)}, u32[]{:S(2)}, u32[]{:S(2)}) collective-permute-start(bf16[1024,1024]{1,0:T(8,128)(2,1)} %all-gather.4.cloned.1.call-done), channel_id=1, source_target_pairs={{0,2},{2,0},{4,6},{6,4},{8,10},{10,8},{12,14},{14,12},{16,18},{18,... | collective-permute-start | bytes 6291464 | tf_op jit(solution)/shard_map/ppermute | solution.py:278
  45.1 2.8 copy-start.18
  48.2 3.3 copy-start.20
  48.6 0.8 copy-start.6
  48.6 1.0 copy-start.7
  48.6 1.1 copy-start.9
  48.7 2.0 copy-start.8
  54.5 3.3 copy-start.14
  57.8 1.7 copy-start.2
  57.8 1.7 copy-start.3
  58.2 0.8 copy-start.13
  58.2 0.9 copy-start.10
  58.2 1.1 copy-start.11
  58.2 1.3 copy-start.12
  59.1 2.1 copy-start.4
  59.5 1.7 copy-start.5
  59.5 2.5 copy-start.21
  61.2 240.5 %all-gather.8.cloned.1.call-start = ((), (), s32[]{:S(2)}) async-start(), calls=%async_computation.2 | async-start | bytes 8912896 | tf_op jit(solution)/shard_map/all_gather | solution.py:258
  75.8 39.8 %collective-permute-start.1 = (bf16[2,8,256,128]{3,2,1,0:T(8,128)(2,1)}, bf16[2,8,256,128]{3,2,1,0:T(8,128)(2,1)}, u32[]{:S(2)}, u32[]{:S(2)}) collective-permute-start(bf16[2,8,256,128]{3,2,1,0:T(8,128)(2,1)} %get-tuple-element.43), channel_id=1, source_target_pairs={{0,2},{2,4},{4,6},{6,8},{8,10},{10,12},{12,14},{14,16},{16,18},{18... | collective-permute-start | bytes 3145736 | tf_op jit(solution)/shard_map/ppermute | solution.py:21
  82.2 91.0 %collective-permute-start.2 = (bf16[2,8,256,128]{3,2,1,0:T(8,128)(2,1)}, bf16[2,8,256,128]{3,2,1,0:T(8,128)(2,1)S(1)}, u32[]{:S(2)}, u32[]{:S(2)}) collective-permute-start(bf16[2,8,256,128]{3,2,1,0:T(8,128)(2,1)} %get-tuple-element.43), channel_id=1, source_target_pairs={{0,4},{2,6},{4,8},{6,10},{8,12},{10,14},{12,16},{14,18},{16,20},{1... | collective-permute-start | bytes 3145736 | tf_op jit(solution)/shard_map/ppermute | solution.py:21
  85.3 96.9 %collective-permute-start.3 = (bf16[2,8,256,128]{3,2,1,0:T(8,128)(2,1)}, bf16[2,8,256,128]{3,2,1,0:T(8,128)(2,1)S(1)}, u32[]{:S(2)}, u32[]{:S(2)}) collective-permute-start(bf16[2,8,256,128]{3,2,1,0:T(8,128)(2,1)} %get-tuple-element.43), channel_id=1, source_target_pairs={{0,6},{2,8},{4,10},{6,12},{8,14},{10,16},{12,18},{14,20},{16,22},{... | collective-permute-start | bytes 3145736 | tf_op jit(solution)/shard_map/ppermute | solution.py:21
  88.0 111.7 %collective-permute-start.4 = (bf16[2,8,256,128]{3,2,1,0:T(8,128)(2,1)}, bf16[2,8,256,128]{3,2,1,0:T(8,128)(2,1)S(1)}, u32[]{:S(2)}, u32[]{:S(2)}) collective-permute-start(bf16[2,8,256,128]{3,2,1,0:T(8,128)(2,1)} %get-tuple-element.43), channel_id=1, source_target_pairs={{0,8},{2,10},{4,12},{6,14},{8,16},{10,18},{12,20},{14,22},{16,24},... | collective-permute-start | bytes 3145736 | tf_op jit(solution)/shard_map/ppermute | solution.py:21
  92.8 107.0 %collective-permute-start.5 = (bf16[2,8,256,128]{3,2,1,0:T(8,128)(2,1)S(1)}, bf16[2,8,256,128]{3,2,1,0:T(8,128)(2,1)S(1)}, u32[]{:S(2)}, u32[]{:S(2)}) collective-permute-start(bf16[2,8,256,128]{3,2,1,0:T(8,128)(2,1)S(1)} %get-tuple-element.37), channel_id=1, source_target_pairs={{2,0},{4,2},{6,4},{8,6},{10,8},{12,10},{14,12},{16,14},{18,16},{20... | collective-permute-start | bytes 3145736 | tf_op jit(solution)/shard_map/ppermute | solution.py:21
  95.9 88.6 %slice-start = ((s8[5242880]{0:T(1024)(128)(4,1)}), s8[4194304]{0:T(1024)(128)(4,1)S(1)}, s32[]{:S(2)}) async-start(s8[5242880]{0:T(1024)(128)(4,1)} %bitcast.279), calls=%async_computation.3 | async-start | bytes 8388608
  97.7 86.7 %slice-start.1 = ((s8[5242880]{0:T(1024)(128)(4,1)}), s8[1048576]{0:T(1024)(128)(4,1)S(1)}, s32[]{:S(2)}) async-start(s8[5242880]{0:T(1024)(128)(4,1)} %bitcast.279), calls=%async_computation.4 | async-start | bytes 2097152
  115.6 84.3 %collective-permute-start.6 = (bf16[2,8,256,128]{3,2,1,0:T(8,128)(2,1)S(1)}, bf16[2,8,256,128]{3,2,1,0:T(8,128)(2,1)S(1)}, u32[]{:S(2)}, u32[]{:S(2)}) collective-permute-start(bf16[2,8,256,128]{3,2,1,0:T(8,128)(2,1)S(1)} %get-tuple-element.37), channel_id=1, source_target_pairs={{4,0},{6,2},{8,4},{10,6},{12,8},{14,10},{16,12},{18,14},{20,16},{2... | collective-permute-start | bytes 3145736 | tf_op jit(solution)/shard_map/ppermute | solution.py:21
  173.2 37.0 %collective-permute-start.7 = (bf16[2,8,256,128]{3,2,1,0:T(8,128)(2,1)S(1)}, bf16[2,8,256,128]{3,2,1,0:T(8,128)(2,1)S(1)}, u32[]{:S(2)}, u32[]{:S(2)}) collective-permute-start(bf16[2,8,256,128]{3,2,1,0:T(8,128)(2,1)S(1)} %get-tuple-element.37), channel_id=1, source_target_pairs={{6,0},{8,2},{10,4},{12,6},{14,8},{16,10},{18,12},{20,14},{22,16},{... | collective-permute-start | bytes 3145736 | tf_op jit(solution)/shard_map/ppermute | solution.py:21
  182.2 36.2 %collective-permute-start.8 = (bf16[2,8,256,128]{3,2,1,0:T(8,128)(2,1)S(1)}, bf16[2,8,256,128]{3,2,1,0:T(8,128)(2,1)S(1)}, u32[]{:S(2)}, u32[]{:S(2)}) collective-permute-start(bf16[2,8,256,128]{3,2,1,0:T(8,128)(2,1)S(1)} %get-tuple-element.37), channel_id=1, source_target_pairs={{8,0},{10,2},{12,4},{14,6},{16,8},{18,10},{20,12},{22,14},{24,16},... | collective-permute-start | bytes 3145736 | tf_op jit(solution)/shard_map/ppermute | solution.py:21
  259.8 70.1 %collective-permute-start.9 = (f32[8,3,256]{2,1,0:T(4,128)S(1)}, f32[8,3,256]{2,1,0:T(4,128)S(1)}, u32[]{:S(2)}, u32[]{:S(2)}) collective-permute-start(f32[8,3,256]{2,1,0:T(4,128)S(1)} %copy.327), channel_id=1, source_target_pairs={{2,0},{4,2},{6,4},{8,6},{10,8},{12,10},{14,12},{16,14},{18,16},{20... | collective-permute-start | bytes 73736 | tf_op jit(solution)/shard_map/ppermute | solution.py:21
  285.7 44.3 %collective-permute-start.10 = (f32[8,3,256]{2,1,0:T(4,128)S(1)}, f32[8,3,256]{2,1,0:T(4,128)S(1)}, u32[]{:S(2)}, u32[]{:S(2)}) collective-permute-start(f32[8,3,256]{2,1,0:T(4,128)S(1)} %copy.327), channel_id=1, source_target_pairs={{4,0},{6,2},{8,4},{10,6},{12,8},{14,10},{16,12},{18,14},{20,16},{2... | collective-permute-start | bytes 73736 | tf_op jit(solution)/shard_map/ppermute | solution.py:21
  298.4 31.6 %collective-permute-start.11 = (f32[8,3,256]{2,1,0:T(4,128)S(1)}, f32[8,3,256]{2,1,0:T(4,128)S(1)}, u32[]{:S(2)}, u32[]{:S(2)}) collective-permute-start(f32[8,3,256]{2,1,0:T(4,128)S(1)} %copy.327), channel_id=1, source_target_pairs={{6,0},{8,2},{10,4},{12,6},{14,8},{16,10},{18,12},{20,14},{22,16},{... | collective-permute-start | bytes 73736 | tf_op jit(solution)/shard_map/ppermute | solution.py:21
  300.3 29.7 %collective-permute-start.12 = (f32[8,3,256]{2,1,0:T(4,128)S(1)}, f32[8,3,256]{2,1,0:T(4,128)S(1)}, u32[]{:S(2)}, u32[]{:S(2)}) collective-permute-start(f32[8,3,256]{2,1,0:T(4,128)S(1)} %copy.327), channel_id=1, source_target_pairs={{8,0},{10,2},{12,4},{14,6},{16,8},{18,10},{20,12},{22,14},{24,16},... | collective-permute-start | bytes 73736 | tf_op jit(solution)/shard_map/ppermute | solution.py:21
  330.0 0.7 copy-start.19
  356.0 1.6 copy-start.15
  356.0 1.6 copy-start.16
  357.8 6.1 %copy-start.1 = (bf16[1,512,2048]{2,1,0:T(8,128)(2,1)S(1)}, bf16[1,512,2048]{2,1,0:T(8,128)(2,1)}, u32[]{:S(2)}) copy-start(bf16[1,512,2048]{2,1,0:T(8,128)(2,1)} %param.11) | copy-start | bytes 6291460
Sparse Core Ops, SparseCore 0:
  10.1 34.1 all-gather.3
  61.4 140.1 all-gather.5
  203.7 83.1 all-gather.7

commit v3 on v2

--- a/solution.py
+++ b/solution.py
@@ -208,16 +208,28 @@
     return pl.BlockSpec((1,) + tuple(shape[1:]), lambda h: (h,) + (0,) * (len(shape) - 1))
 
 
+def per_head_of(operand):
+    if isinstance(operand, tuple):
+        stacked, index = operand
+        rest = (0,) * (stacked.ndim - 2)
+        spec = pl.BlockSpec(
+            (pl.Squeezed(), 1) + tuple(stacked.shape[2:]), lambda h: (index, h) + rest
+        )
+        return spec, stacked
+    return per_head(operand.shape), operand
+
+
 def run_per_head(kernel, inputs, out_shapes):
-    heads = inputs[0].shape[0]
+    heads = out_shapes[0].shape[0]
+    specs, arrays = zip(*[per_head_of(x) for x in inputs])
     return pl.pallas_call(
         kernel,
         grid=(heads,),
-        in_specs=[per_head(x.shape) for x in inputs],
+        in_specs=list(specs),
         out_specs=[per_head(s.shape) for s in out_shapes],
         out_shape=out_shapes,
         compiler_params=pltpu.CompilerParams(dimension_semantics=("arbitrary",)),
-    )(*inputs)
+    )(*arrays)
 
 
 def column(x):
@@ -311,10 +323,10 @@
         [
             order_rows(q_rows, par_long),
             order_rows(g_rows, par_long),
-            near_kv[0],
-            near_kv[1],
-            all_kv_long[0],
-            all_kv_long[1],
+            (near_kv, 0),
+            (near_kv, 1),
+            (all_kv_long, 0),
+            (all_kv_long, 1),
             column(order_last(own_pos, par_long)),
             column(order_last(own_seg_short, par_long)),
             column(order_last(own_seg_long, par_long)),
@@ -339,15 +351,16 @@
     query_seg_short = jnp.where(
         query_pos_short < total, segment_of(query_pos_short, segments_short), -2
     )
+    ordered_kv = order_rows(own_kv, par_long)
     grad_key, grad_value = run_per_head(
         functools.partial(key_kernel, scale=scale),
         [
-            order_rows(own_kv[0], par_long),
-            order_rows(own_kv[1], par_long),
-            near_qg[0],
-            near_qg[1],
-            all_qg_long[0],
-            all_qg_long[1],
+            (ordered_kv, 0),
+            (ordered_kv, 1),
+            (near_qg, 0),
+            (near_qg, 1),
+            (all_qg_long, 0),
+            (all_qg_long, 1),
             column(order_last(own_pos, par_long)),
             column(order_last(own_seg_short, par_long)),
             column(order_last(own_seg_long, par_long)),

time: 375 us -> 376 us (level)
  blocking collectives: 22.4 us -> 32.3 us
  waiting for transfers between devices: 145 us -> 137 us
    squeeze x4 -> x0, local copies, waits for them, and re-layouts: 17.2 us -> none  [the longest x1 5.89 us: shards(): all_kv_long[1]]
    unnamed x77 -> x75, local copies, waits for them, and re-layouts: 10.6 us -> 21 us
    all_gather x1, blocking collectives: 22.4 us -> 32.3 us  [shards(): lax.all_gather(take_stats(own_stats, par_long), 'seq', axis=2, tiled=True)]
    ppermute x12, waiting for transfers between devices: 109 us -> 101 us  [passed_along(): return lax.ppermute(value, axis, pairs)]
  transfers between devices with their start and end apart: 16 -> 16, of which waited for: 7 -> 7; matrix products, arithmetic and copies ran while one was open for 15% -> 14% of each run, Pallas kernels for 7% -> 7%
where the time goes in v3:
time: 376 us; the launch traced here: 370 us
  waiting for transfers between devices  137 us (36%)
  starting transfers between devices  64.1 us (17%)
  Pallas kernels  44 us (12%)
  local copies, waits for them, and re-layouts  42.2 us (11%)
  blocking collectives  32.3 us (9%)
  other arithmetic  29.4 us (8%)
  between operations  15.2 us (4%)
  matrix products  5.92 us (2%)
    ppermute x12, waiting for transfers between devices, passed_along(): return lax.ppermute(value, axis, pairs)  101 us
    ppermute x12, starting transfers between devices, passed_along(): return lax.ppermute(value, axis, pairs)  63.1 us
    pallas_call x2, Pallas kernels, run_per_head(): pl.pallas_call(kernel, grid=(heads,), in_specs=list(specs), out_specs=[pe...  44 us
    all_gather x1, waiting for transfers between devices, shards(): lax.all_gather(lax.dynamic_slice_in_dim(out_weight, core * half_width, ha...  34.5 us
    all_gather x1, blocking collectives, shards(): lax.all_gather(take_stats(own_stats, par_long), 'seq', axis=2, tiled=True)  32.3 us
    unnamed x75, local copies, waits for them, and re-layouts  21 us
  transfers between devices with their start and end apart: 16, of which 7 were waited for; matrix products, arithmetic and copies ran while one was open for 14% of the time, Pallas kernels for 7%

profile of v3, /device:TPU:5, one launch (start us, length us, event | category | flops | bytes accessed | tf_op | source)
XLA Modules:
  0.0 369.8 jit_solution(11431832290937486907)
XLA Ops:
  7.2 2.4 constant_dynamic-slice_fusion
  9.7 34.5 %all-gather.4.cloned.1.call-done = bf16[1024,1024]{1,0:T(8,128)(2,1)} async-done(((bf16[512,1024]{1,0:T(8,128)(2,1)}), bf16[1024,1024]{1,0:T(8,128)(2,1)}) %all-gather.4.cloned.1.call-update) | async-done | bytes 2097168 | tf_op jit(solution)/shard_map/all_gather | solution.py:284
  45.1 1.6 copy.338
  48.0 1.5 copy.341
  53.7 2.9 fusion.5
  56.6 3.0 fusion
  61.8 1.5 broadcast_select_fusion
  68.7 3.9 %bitcast_select_fusion.5 = (bf16[1,8,256,128]{3,2,1,0:T(8,128)(2,1)}, bf16[1,8,256,128]{3,2,1,0:T(8,128)(2,1)S(1)}, bf16[1,8,256,128]{3,2,1,0:T(8,128)(2,1)}, bf16[1,8,256,128]{3,2,1,0:T(8,128)(2,1)S(1)}) fusion(pred[8]{0:T(512)(128)(4,1)S(1)} %broadcast_compare_fusion.3, bf16[8,256,1,128]{3,0,2,1:T(8,128)(2,1)S(1)} %copy-done.5, ...), kind=kLoop, calls=%fused_computation.41 | loop fusion | flops 1048576 | bytes 6291464 | tf_op jit(solution)/shard_map/jit(_where)/select_n | solution.py:27
  72.7 1.9 pad_maximum_fusion
  74.5 3.0 collective-permute-start.1
  77.6 3.1 collective-permute-start.2
  80.8 2.7 collective-permute-start.3
  83.5 1.3 copy.276.qpos_ref.kpos_ref
  84.8 1.3 copy.277.qss_ref.kss_ref
  86.2 1.3 copy.278.qsl_ref.ksl_ref
  89.5 3.2 collective-permute-start.4
  92.7 2.3 pad_maximum_fusion.3
  95.0 3.0 collective-permute-start.5
  98.2 17.0 %collective-permute-done.1 = bf16[2,8,256,128]{3,2,1,0:T(8,128)(2,1)} collective-permute-done((bf16[2,8,256,128]{3,2,1,0:T(8,128)(2,1)}, bf16[2,8,256,128]{3,2,1,0:T(8,128)(2,1)}, u32[]{:S(2)}, u32[]{:S(2)}) %collective-permute-start.1) | collective-permute-done | bytes 1048608 | tf_op jit(solution)/shard_map/ppermute | solution.py:21
  115.2 1.9 collective-permute-start.6
  117.3 57.5 %collective-permute-done.2 = bf16[2,8,256,128]{3,2,1,0:T(8,128)(2,1)} collective-permute-done((bf16[2,8,256,128]{3,2,1,0:T(8,128)(2,1)}, bf16[2,8,256,128]{3,2,1,0:T(8,128)(2,1)}, u32[]{:S(2)}, u32[]{:S(2)}) %collective-permute-start.2) | collective-permute-done | bytes 1048608 | tf_op jit(solution)/shard_map/ppermute | solution.py:21
  174.8 1.9 collective-permute-start.7
  177.8 3.6 collective-permute-done.3
  181.4 1.5 collective-permute-start.8
  184.0 2.4 constant_dynamic-update-slice_fusion.3
  186.4 2.4 constant_dynamic-update-slice_fusion.2
  188.8 2.4 constant_dynamic-update-slice_fusion.1
  191.3 10.3 %collective-permute-done.4 = bf16[2,8,256,128]{3,2,1,0:T(8,128)(2,1)S(1)} collective-permute-done((bf16[2,8,256,128]{3,2,1,0:T(8,128)(2,1)}, bf16[2,8,256,128]{3,2,1,0:T(8,128)(2,1)S(1)}, u32[]{:S(2)}, u32[]{:S(2)}) %collective-permute-start.4) | collective-permute-done | bytes 1048608 | tf_op jit(solution)/shard_map/ppermute | solution.py:21
  205.1 7.6 %collective-permute-done.7 = bf16[2,8,256,128]{3,2,1,0:T(8,128)(2,1)S(1)} collective-permute-done((bf16[2,8,256,128]{3,2,1,0:T(8,128)(2,1)S(1)}, bf16[2,8,256,128]{3,2,1,0:T(8,128)(2,1)S(1)}, u32[]{:S(2)}, u32[]{:S(2)}) %collective-permute-start.7) | collective-permute-done | bytes 1048608 | tf_op jit(solution)/shard_map/ppermute | solution.py:21
  212.6 1.2 constant_dynamic-update-slice_fusion.16
  213.9 5.4 %collective-permute-done.8 = bf16[2,8,256,128]{3,2,1,0:T(8,128)(2,1)S(1)} collective-permute-done((bf16[2,8,256,128]{3,2,1,0:T(8,128)(2,1)S(1)}, bf16[2,8,256,128]{3,2,1,0:T(8,128)(2,1)S(1)}, u32[]{:S(2)}, u32[]{:S(2)}) %collective-permute-start.8) | collective-permute-done | bytes 1048608 | tf_op jit(solution)/shard_map/ppermute | solution.py:21
  220.5 24.6 %shard_map.103 = (f32[8,256,128]{2,1,0:T(8,128)}, f32[8,256,1]{2,1,0:T(8,128)}, f32[8,256,1]{2,1,0:T(8,128)}, f32[8,256,1]{2,1,0:T(8,128)}) custom-call(bf16[8,256,128]{2,1,0:T(8,128)(2,1)} %get-tuple-element.119.q_ref, bf16[8,256,128]{2,1,0:T(8,128)(2,1)} %get-tuple-element.120.g_ref, ...), custom_call_target="tpu_custom_call" | custom-call | tf_op jit(solution)/shard_map/pallas_call | solution.py:225
  245.1 1.6 reduce.2
  246.6 1.6 reduce.1
  248.2 1.9 reduce
  250.7 26.0 %collective-permute-start.9 = (f32[8,3,256]{2,1,0:T(4,128)S(1)}, f32[8,3,256]{2,1,0:T(4,128)S(1)}, u32[]{:S(2)}, u32[]{:S(2)}) collective-permute-start(f32[8,3,256]{2,1,0:T(4,128)S(1)} %copy.303), channel_id=1, source_target_pairs={{2,0},{4,2},{6,4},{8,6},{10,8},{12,10},{14,12},{16,14},{18,16},{20... | collective-permute-start | bytes 73736 | tf_op jit(solution)/shard_map/ppermute | solution.py:21
  276.7 13.7 %collective-permute-start.10 = (f32[8,3,256]{2,1,0:T(4,128)S(1)}, f32[8,3,256]{2,1,0:T(4,128)S(1)}, u32[]{:S(2)}, u32[]{:S(2)}) collective-permute-start(f32[8,3,256]{2,1,0:T(4,128)S(1)} %copy.303), channel_id=1, source_target_pairs={{4,0},{6,2},{8,4},{10,6},{12,8},{14,10},{16,12},{18,14},{20,16},{2... | collective-permute-start | bytes 73736 | tf_op jit(solution)/shard_map/ppermute | solution.py:21
  290.4 1.9 collective-permute-start.11
  292.3 1.3 collective-permute-start.12
  293.7 32.3 %all_gather.15.stl_ref = f32[8,3,2048]{2,1,0:T(4,128)} all-gather(f32[8,3,128]{2,1,0:T(4,128)S(1)} %fusion.16), channel_id=1, replica_groups=mesh['seq'=16,'fsdp'=2] {'seq'}, dimensions={2}, use_global_device_ids=true | all-gather | bytes 208896 | tf_op jit(solution)/shard_map/all_gather | solution.py:346
  326.8 19.4 %shard_map.104 = (f32[8,256,128]{2,1,0:T(8,128)}, f32[8,256,128]{2,1,0:T(8,128)}) custom-call(bf16[2,8,256,128]{3,2,1,0:T(8,128)(2,1)} %pad_maximum_fusion.2.k_ref.v_ref, bf16[2,8,256,128]{3,2,1,0:T(8,128)(2,1)} %pad_maximum_fusion.2.k_ref.v_ref, bf16[2,8,1280,128]{3,2,1,0:T(8,128)(2,1)} %constant_dynamic-update-slice_fusion.15.qs_ref.gs_ref, ...), custom_call_target="tpu_custom_call" | custom-call | tf_op jit(solution)/shard_map/pallas_call | solution.py:225
  346.3 2.9 select_bitcast_fusion.9
  350.6 1.5 bitcast_select_fusion.7
  352.4 1.3 reshape.964
  353.6 1.4 pad_maximum_fusion.4
  356.2 2.3 reshape.966
  358.5 1.3 pad_maximum_fusion.5
  361.0 2.3 reshape.968
  (158 shorter events, 27.8 us)
Async XLA Ops:
  7.2 46.5 %copy-start = (bf16[1,512,2048]{2,1,0:T(8,128)(2,1)S(1)}, bf16[1,512,2048]{2,1,0:T(8,128)(2,1)}, u32[]{:S(2)}) copy-start(bf16[1,512,2048]{2,1,0:T(8,128)(2,1)} %param.11) | copy-start | bytes 6291460
  7.2 37.1 %all-gather.4.cloned.1.call-start = ((), (), s32[]{:S(2)}) async-start(), calls=%async_computation | async-start | bytes 3145728 | tf_op jit(solution)/shard_map/all_gather | solution.py:284
  9.7 210.8 %all-gather.6.cloned.1.call-start = ((), (), s32[]{:S(2)}) async-start(), calls=%async_computation.1 | async-start | bytes 8912896 | tf_op jit(solution)/shard_map/all_gather | solution.py:270
  44.3 12.3 %collective-permute-start = (bf16[1024,1024]{1,0:T(8,128)(2,1)}, bf16[1024,1024]{1,0:T(8,128)(2,1)}, u32[]{:S(2)}, u32[]{:S(2)}) collective-permute-start(bf16[1024,1024]{1,0:T(8,128)(2,1)} %all-gather.4.cloned.1.call-done), channel_id=1, source_target_pairs={{0,2},{2,0},{4,6},{6,4},{8,10},{10,8},{12,14},{14,12},{16,18},{18,... | collective-permute-start | bytes 6291464 | tf_op jit(solution)/shard_map/ppermute | solution.py:290
  45.1 2.6 copy-start.19
  46.8 0.8 copy-start.2
  46.8 1.0 copy-start.4
  48.0 5.6 %copy-start.21 = (s32[8]{0:T(128)S(1)}, s32[8]{0:T(128)}, u32[]{:S(2)}) copy-start(s32[8]{0:T(128)} %param.13) | copy-start | bytes 100
  49.9 1.9 copy-start.10
  49.9 2.8 copy-start.11
  49.9 2.8 copy-start.9
  49.9 2.8 copy-start.12
  56.6 4.4 %copy-start.13 = (bf16[8,256,1,128]{3,1,0,2:T(8,128)(2,1)S(1)}, bf16[8,256,1,128]{3,1,0,2:T(8,128)(2,1)}, u32[]{:S(2)}) copy-start(bf16[8,256,1,128]{3,1,0,2:T(8,128)(2,1)} %copy.335) | copy-start | bytes 1572868
  56.6 4.4 %copy-start.14 = (bf16[8,256,1,128]{3,1,0,2:T(8,128)(2,1)S(1)}, bf16[8,256,1,128]{3,1,0,2:T(8,128)(2,1)}, u32[]{:S(2)}) copy-start(bf16[8,256,1,128]{3,1,0,2:T(8,128)(2,1)} %copy.334) | copy-start | bytes 1572868
  56.6 4.4 %copy-start.15 = (bf16[8,256,1,128]{3,1,0,2:T(8,128)(2,1)S(1)}, bf16[8,256,1,128]{3,1,0,2:T(8,128)(2,1)}, u32[]{:S(2)}) copy-start(bf16[8,256,1,128]{3,1,0,2:T(8,128)(2,1)} %copy.333) | copy-start | bytes 1572868
  56.6 4.4 %copy-start.16 = (bf16[8,256,1,128]{3,1,0,2:T(8,128)(2,1)S(1)}, bf16[8,256,1,128]{3,1,0,2:T(8,128)(2,1)}, u32[]{:S(2)}) copy-start(bf16[8,256,1,128]{3,1,0,2:T(8,128)(2,1)} %copy.332) | copy-start | bytes 1572868
  60.0 0.8 copy-start.7
  60.0 1.0 copy-start.6
  61.0 3.6 copy-start.22
  61.0 7.7 %copy-start.3 = (bf16[8,256,1,128]{3,0,2,1:T(8,128)(2,1)S(1)}, bf16[8,256,1,128]{3,0,2,1:T(8,128)(2,1)}, u32[]{:S(2)}) copy-start(bf16[8,256,1,128]{3,0,2,1:T(8,128)(2,1)} %copy-done.2) | copy-start | bytes 1572868
  61.0 7.7 %copy-start.5 = (bf16[8,256,1,128]{3,0,2,1:T(8,128)(2,1)S(1)}, bf16[8,256,1,128]{3,0,2,1:T(8,128)(2,1)}, u32[]{:S(2)}) copy-start(bf16[8,256,1,128]{3,0,2,1:T(8,128)(2,1)} %copy-done.4) | copy-start | bytes 1572868
  63.2 263.0 %all-gather.8.cloned.1.call-start = ((), (), s32[]{:S(2)}) async-start(), calls=%async_computation.2 | async-start | bytes 8912896 | tf_op jit(solution)/shard_map/all_gather | solution.py:270
  72.7 20.0 %copy-start.17 = (bf16[1,8,256,128]{3,2,1,0:T(8,128)(2,1)S(1)}, bf16[1,8,256,128]{3,2,1,0:T(8,128)(2,1)}, u32[]{:S(2)}) copy-start(bf16[1,8,256,128]{3,2,1,0:T(8,128)(2,1)} %get-tuple-element.108) | copy-start | bytes 1572868
  74.5 40.7 %collective-permute-start.1 = (bf16[2,8,256,128]{3,2,1,0:T(8,128)(2,1)}, bf16[2,8,256,128]{3,2,1,0:T(8,128)(2,1)}, u32[]{:S(2)}, u32[]{:S(2)}) collective-permute-start(bf16[2,8,256,128]{3,2,1,0:T(8,128)(2,1)} %get-tuple-element.37), channel_id=1, source_target_pairs={{0,2},{2,4},{4,6},{6,8},{8,10},{10,12},{12,14},{14,16},{16,18},{18... | collective-permute-start | bytes 3145736 | tf_op jit(solution)/shard_map/ppermute | solution.py:21
  77.6 97.2 %collective-permute-start.2 = (bf16[2,8,256,128]{3,2,1,0:T(8,128)(2,1)}, bf16[2,8,256,128]{3,2,1,0:T(8,128)(2,1)}, u32[]{:S(2)}, u32[]{:S(2)}) collective-permute-start(bf16[2,8,256,128]{3,2,1,0:T(8,128)(2,1)} %get-tuple-element.37), channel_id=1, source_target_pairs={{0,4},{2,6},{4,8},{6,10},{8,12},{10,14},{12,16},{14,18},{16,20},{1... | collective-permute-start | bytes 3145736 | tf_op jit(solution)/shard_map/ppermute | solution.py:21
  80.8 100.7 %collective-permute-start.3 = (bf16[2,8,256,128]{3,2,1,0:T(8,128)(2,1)}, bf16[2,8,256,128]{3,2,1,0:T(8,128)(2,1)}, u32[]{:S(2)}, u32[]{:S(2)}) collective-permute-start(bf16[2,8,256,128]{3,2,1,0:T(8,128)(2,1)} %get-tuple-element.37), channel_id=1, source_target_pairs={{0,6},{2,8},{4,10},{6,12},{8,14},{10,16},{12,18},{14,20},{16,22},{... | collective-permute-start | bytes 3145736 | tf_op jit(solution)/shard_map/ppermute | solution.py:21
  84.8 91.8 %copy-start.8 = (bf16[2,8,128,128]{3,2,1,0:T(8,128)(2,1)S(1)}, bf16[2,8,128,128]{3,2,1,0:T(8,128)(2,1)}, u32[]{:S(2)}) copy-start(bf16[2,8,128,128]{3,2,1,0:T(8,128)(2,1)} %get-tuple-element.32) | copy-start | bytes 1572868
  87.5 89.2 %copy-start.18 = (bf16[2,8,128,128]{3,2,1,0:T(8,128)(2,1)S(1)}, bf16[2,8,128,128]{3,2,1,0:T(8,128)(2,1)}, u32[]{:S(2)}) copy-start(bf16[2,8,128,128]{3,2,1,0:T(8,128)(2,1)} %get-tuple-element.31) | copy-start | bytes 1572868
  89.5 112.1 %collective-permute-start.4 = (bf16[2,8,256,128]{3,2,1,0:T(8,128)(2,1)}, bf16[2,8,256,128]{3,2,1,0:T(8,128)(2,1)S(1)}, u32[]{:S(2)}, u32[]{:S(2)}) collective-permute-start(bf16[2,8,256,128]{3,2,1,0:T(8,128)(2,1)} %get-tuple-element.37), channel_id=1, source_target_pairs={{0,8},{2,10},{4,12},{6,14},{8,16},{10,18},{12,20},{14,22},{16,24},... | collective-permute-start | bytes 3145736 | tf_op jit(solution)/shard_map/ppermute | solution.py:21
  95.0 107.7 %collective-permute-start.5 = (bf16[2,8,256,128]{3,2,1,0:T(8,128)(2,1)S(1)}, bf16[2,8,256,128]{3,2,1,0:T(8,128)(2,1)S(1)}, u32[]{:S(2)}, u32[]{:S(2)}) collective-permute-start(bf16[2,8,256,128]{3,2,1,0:T(8,128)(2,1)S(1)} %get-tuple-element.29), channel_id=1, source_target_pairs={{2,0},{4,2},{6,4},{8,6},{10,8},{12,10},{14,12},{16,14},{18,16},{20... | collective-permute-start | bytes 3145736 | tf_op jit(solution)/shard_map/ppermute | solution.py:21
  115.2 88.7 %collective-permute-start.6 = (bf16[2,8,256,128]{3,2,1,0:T(8,128)(2,1)S(1)}, bf16[2,8,256,128]{3,2,1,0:T(8,128)(2,1)S(1)}, u32[]{:S(2)}, u32[]{:S(2)}) collective-permute-start(bf16[2,8,256,128]{3,2,1,0:T(8,128)(2,1)S(1)} %get-tuple-element.29), channel_id=1, source_target_pairs={{4,0},{6,2},{8,4},{10,6},{12,8},{14,10},{16,12},{18,14},{20,16},{2... | collective-permute-start | bytes 3145736 | tf_op jit(solution)/shard_map/ppermute | solution.py:21
  174.8 37.9 %collective-permute-start.7 = (bf16[2,8,256,128]{3,2,1,0:T(8,128)(2,1)S(1)}, bf16[2,8,256,128]{3,2,1,0:T(8,128)(2,1)S(1)}, u32[]{:S(2)}, u32[]{:S(2)}) collective-permute-start(bf16[2,8,256,128]{3,2,1,0:T(8,128)(2,1)S(1)} %get-tuple-element.29), channel_id=1, source_target_pairs={{6,0},{8,2},{10,4},{12,6},{14,8},{16,10},{18,12},{20,14},{22,16},{... | collective-permute-start | bytes 3145736 | tf_op jit(solution)/shard_map/ppermute | solution.py:21
  181.4 37.8 %collective-permute-start.8 = (bf16[2,8,256,128]{3,2,1,0:T(8,128)(2,1)S(1)}, bf16[2,8,256,128]{3,2,1,0:T(8,128)(2,1)S(1)}, u32[]{:S(2)}, u32[]{:S(2)}) collective-permute-start(bf16[2,8,256,128]{3,2,1,0:T(8,128)(2,1)S(1)} %get-tuple-element.29), channel_id=1, source_target_pairs={{8,0},{10,2},{12,4},{14,6},{16,8},{18,10},{20,12},{22,14},{24,16},... | collective-permute-start | bytes 3145736 | tf_op jit(solution)/shard_map/ppermute | solution.py:21
  250.7 75.4 %collective-permute-start.9 = (f32[8,3,256]{2,1,0:T(4,128)S(1)}, f32[8,3,256]{2,1,0:T(4,128)S(1)}, u32[]{:S(2)}, u32[]{:S(2)}) collective-permute-start(f32[8,3,256]{2,1,0:T(4,128)S(1)} %copy.303), channel_id=1, source_target_pairs={{2,0},{4,2},{6,4},{8,6},{10,8},{12,10},{14,12},{16,14},{18,16},{20... | collective-permute-start | bytes 73736 | tf_op jit(solution)/shard_map/ppermute | solution.py:21
  276.7 49.4 %collective-permute-start.10 = (f32[8,3,256]{2,1,0:T(4,128)S(1)}, f32[8,3,256]{2,1,0:T(4,128)S(1)}, u32[]{:S(2)}, u32[]{:S(2)}) collective-permute-start(f32[8,3,256]{2,1,0:T(4,128)S(1)} %copy.303), channel_id=1, source_target_pairs={{4,0},{6,2},{8,4},{10,6},{12,8},{14,10},{16,12},{18,14},{20,16},{2... | collective-permute-start | bytes 73736 | tf_op jit(solution)/shard_map/ppermute | solution.py:21
  290.4 35.7 %collective-permute-start.11 = (f32[8,3,256]{2,1,0:T(4,128)S(1)}, f32[8,3,256]{2,1,0:T(4,128)S(1)}, u32[]{:S(2)}, u32[]{:S(2)}) collective-permute-start(f32[8,3,256]{2,1,0:T(4,128)S(1)} %copy.303), channel_id=1, source_target_pairs={{6,0},{8,2},{10,4},{12,6},{14,8},{16,10},{18,12},{20,14},{22,16},{... | collective-permute-start | bytes 73736 | tf_op jit(solution)/shard_map/ppermute | solution.py:21
  292.3 33.8 %collective-permute-start.12 = (f32[8,3,256]{2,1,0:T(4,128)S(1)}, f32[8,3,256]{2,1,0:T(4,128)S(1)}, u32[]{:S(2)}, u32[]{:S(2)}) collective-permute-start(f32[8,3,256]{2,1,0:T(4,128)S(1)} %copy.303), channel_id=1, source_target_pairs={{8,0},{10,2},{12,4},{14,6},{16,8},{18,10},{20,12},{22,14},{24,16},... | collective-permute-start | bytes 73736 | tf_op jit(solution)/shard_map/ppermute | solution.py:21
  326.2 0.7 copy-start.20
  353.6 9.7 %copy-start.1 = (bf16[1,512,2048]{2,1,0:T(8,128)(2,1)S(1)}, bf16[1,512,2048]{2,1,0:T(8,128)(2,1)}, u32[]{:S(2)}) copy-start(bf16[1,512,2048]{2,1,0:T(8,128)(2,1)} %param.11) | copy-start | bytes 6291460
Sparse Core Ops, SparseCore 0:
  10.1 34.1 all-gather.3
  63.4 141.2 all-gather.5
  206.8 81.3 all-gather.7

commit v4 on v3

--- a/solution.py
+++ b/solution.py
@@ -155,7 +155,7 @@
                 (kl_ref[0], vl_ref[0], (kpl_ref[0] <= qpos) & (ksl_ref[0] == qsl_ref[0, lo:hi, :]))
             )
         grad_query, top, inverse, delta = attend_rows(q, g, parts, scale)
-        dq_ref[0, lo:hi, :] = grad_query
+        dq_ref[0, lo:hi, :] = grad_query.astype(dq_ref.dtype)
         top_ref[0, lo:hi, :] = top
         inv_ref[0, lo:hi, :] = inverse
         delta_ref[0, lo:hi, :] = delta
@@ -200,8 +200,8 @@
                 )
             )
         grad_key, grad_value = key_rows(k, v, parts, scale)
-        dk_ref[0, lo:hi, :] = grad_key
-        dv_ref[0, lo:hi, :] = grad_value
+        dk_ref[0, lo:hi, :] = grad_key.astype(dk_ref.dtype)
+        dv_ref[0, lo:hi, :] = grad_value.astype(dv_ref.dtype)
 
 
 def per_head(shape):
@@ -316,7 +316,7 @@
     )
     key_seg_short = jnp.where(key_pos_short >= 0, segment_of(key_pos_short, segments_short), -1)
     f32 = jnp.float32
-    row_shape = jax.ShapeDtypeStruct((head_count, rows_short, head_width), f32)
+    row_shape = jax.ShapeDtypeStruct((head_count, rows_short, head_width), jnp.bfloat16)
     stat_shape = jax.ShapeDtypeStruct((head_count, rows_short, 1), f32)
     grad_query, top, inverse, delta = run_per_head(
         functools.partial(query_kernel, scale=scale),

time: 376 us -> 374 us (level)
    unnamed x75 -> x77, local copies, waits for them, and re-layouts: 21 us -> 21.1 us
where the time goes in v4:
time: 374 us; the launch traced here: 368 us
  waiting for transfers between devices  136 us (36%)
  starting transfers between devices  63.9 us (17%)
  Pallas kernels  44 us (12%)
  local copies, waits for them, and re-layouts  42.5 us (11%)
  blocking collectives  32.1 us (9%)
  other arithmetic  28 us (7%)
  between operations  15.2 us (4%)
  matrix products  5.91 us (2%)
    ppermute x12, waiting for transfers between devices, passed_along(): return lax.ppermute(value, axis, pairs)  101 us
    ppermute x12, starting transfers between devices, passed_along(): return lax.ppermute(value, axis, pairs)  63 us
    pallas_call x2, Pallas kernels, run_per_head(): pl.pallas_call(kernel, grid=(heads,), in_specs=list(specs), out_specs=[pe...  44 us
    all_gather x1, waiting for transfers between devices, shards(): lax.all_gather(lax.dynamic_slice_in_dim(out_weight, core * half_width, ha...  34.5 us
    all_gather x1, blocking collectives, shards(): lax.all_gather(take_stats(own_stats, par_long), 'seq', axis=2, tiled=True)  32.1 us
    unnamed x77, local copies, waits for them, and re-layouts  21.1 us
  transfers between devices with their start and end apart: 16, of which 7 were waited for; matrix products, arithmetic and copies ran while one was open for 14% of the time, Pallas kernels for 7%

profile of v4, /device:TPU:5, one launch (start us, length us, event | category | flops | bytes accessed | tf_op | source)
XLA Modules:
  0.0 368.0 jit_solution(14832579473696928172)
XLA Ops:
  7.2 2.4 constant_dynamic-slice_fusion
  9.7 34.5 %all-gather.4.cloned.1.call-done = bf16[1024,1024]{1,0:T(8,128)(2,1)} async-done(((bf16[512,1024]{1,0:T(8,128)(2,1)}), bf16[1024,1024]{1,0:T(8,128)(2,1)}) %all-gather.4.cloned.1.call-update) | async-done | bytes 2097168 | tf_op jit(solution)/shard_map/all_gather | solution.py:284
  45.1 1.6 copy.338
  48.0 1.5 copy.341
  53.7 2.9 fusion.2
  56.6 3.0 fusion
  61.7 1.5 broadcast_select_fusion
  68.7 3.9 %bitcast_select_fusion.5 = (bf16[1,8,256,128]{3,2,1,0:T(8,128)(2,1)}, bf16[1,8,256,128]{3,2,1,0:T(8,128)(2,1)S(1)}, bf16[1,8,256,128]{3,2,1,0:T(8,128)(2,1)}, bf16[1,8,256,128]{3,2,1,0:T(8,128)(2,1)S(1)}) fusion(pred[8]{0:T(512)(128)(4,1)S(1)} %broadcast_compare_fusion.3, bf16[8,256,1,128]{3,0,2,1:T(8,128)(2,1)S(1)} %copy-done.5, ...), kind=kLoop, calls=%fused_computation.38 | loop fusion | flops 1048576 | bytes 6291464 | tf_op jit(solution)/shard_map/jit(_where)/select_n | solution.py:27
  72.6 1.8 pad_maximum_fusion
  74.5 3.0 collective-permute-start.1
  77.5 3.1 collective-permute-start.2
  80.7 2.7 collective-permute-start.3
  83.5 1.3 copy.276.qpos_ref.kpos_ref
  84.8 1.3 copy.277.qss_ref.kss_ref
  86.2 1.3 copy.278.qsl_ref.ksl_ref
  89.5 3.2 collective-permute-start.4
  92.6 2.3 pad_maximum_fusion.3
  95.0 2.9 collective-permute-start.5
  98.2 16.9 %collective-permute-done.1 = bf16[2,8,256,128]{3,2,1,0:T(8,128)(2,1)} collective-permute-done((bf16[2,8,256,128]{3,2,1,0:T(8,128)(2,1)}, bf16[2,8,256,128]{3,2,1,0:T(8,128)(2,1)}, u32[]{:S(2)}, u32[]{:S(2)}) %collective-permute-start.1) | collective-permute-done | bytes 1048608 | tf_op jit(solution)/shard_map/ppermute | solution.py:21
  115.1 1.9 collective-permute-start.6
  117.3 57.4 %collective-permute-done.2 = bf16[2,8,256,128]{3,2,1,0:T(8,128)(2,1)} collective-permute-done((bf16[2,8,256,128]{3,2,1,0:T(8,128)(2,1)}, bf16[2,8,256,128]{3,2,1,0:T(8,128)(2,1)}, u32[]{:S(2)}, u32[]{:S(2)}) %collective-permute-start.2) | collective-permute-done | bytes 1048608 | tf_op jit(solution)/shard_map/ppermute | solution.py:21
  174.7 1.9 collective-permute-start.7
  177.8 3.7 %collective-permute-done.3 = bf16[2,8,256,128]{3,2,1,0:T(8,128)(2,1)} collective-permute-done((bf16[2,8,256,128]{3,2,1,0:T(8,128)(2,1)}, bf16[2,8,256,128]{3,2,1,0:T(8,128)(2,1)}, u32[]{:S(2)}, u32[]{:S(2)}) %collective-permute-start.3) | collective-permute-done | bytes 1048608 | tf_op jit(solution)/shard_map/ppermute | solution.py:21
  181.4 1.5 collective-permute-start.8
  184.0 2.5 constant_dynamic-update-slice_fusion.3
  186.5 2.4 constant_dynamic-update-slice_fusion.2
  188.9 2.5 constant_dynamic-update-slice_fusion.1
  191.4 10.2 %collective-permute-done.4 = bf16[2,8,256,128]{3,2,1,0:T(8,128)(2,1)S(1)} collective-permute-done((bf16[2,8,256,128]{3,2,1,0:T(8,128)(2,1)}, bf16[2,8,256,128]{3,2,1,0:T(8,128)(2,1)S(1)}, u32[]{:S(2)}, u32[]{:S(2)}) %collective-permute-start.4) | collective-permute-done | bytes 1048608 | tf_op jit(solution)/shard_map/ppermute | solution.py:21
  205.2 7.4 %collective-permute-done.7 = bf16[2,8,256,128]{3,2,1,0:T(8,128)(2,1)S(1)} collective-permute-done((bf16[2,8,256,128]{3,2,1,0:T(8,128)(2,1)S(1)}, bf16[2,8,256,128]{3,2,1,0:T(8,128)(2,1)S(1)}, u32[]{:S(2)}, u32[]{:S(2)}) %collective-permute-start.7) | collective-permute-done | bytes 1048608 | tf_op jit(solution)/shard_map/ppermute | solution.py:21
  212.6 1.2 constant_dynamic-update-slice_fusion.16
  213.8 5.5 %collective-permute-done.8 = bf16[2,8,256,128]{3,2,1,0:T(8,128)(2,1)S(1)} collective-permute-done((bf16[2,8,256,128]{3,2,1,0:T(8,128)(2,1)S(1)}, bf16[2,8,256,128]{3,2,1,0:T(8,128)(2,1)S(1)}, u32[]{:S(2)}, u32[]{:S(2)}) %collective-permute-start.8) | collective-permute-done | bytes 1048608 | tf_op jit(solution)/shard_map/ppermute | solution.py:21
  220.5 24.6 %shard_map.103 = (bf16[8,256,128]{2,1,0:T(8,128)(2,1)}, f32[8,256,1]{2,1,0:T(8,128)}, f32[8,256,1]{2,1,0:T(8,128)}, f32[8,256,1]{2,1,0:T(8,128)}) custom-call(bf16[8,256,128]{2,1,0:T(8,128)(2,1)} %get-tuple-element.119.q_ref, bf16[8,256,128]{2,1,0:T(8,128)(2,1)} %get-tuple-element.120.g_ref, ...), custom_call_target="tpu_custom_call" | custom-call | tf_op jit(solution)/shard_map/pallas_call | solution.py:225
  245.1 1.6 reduce.2
  246.7 1.6 reduce.1
  248.3 1.9 reduce
  250.7 25.9 %collective-permute-start.9 = (f32[8,3,256]{2,1,0:T(4,128)S(1)}, f32[8,3,256]{2,1,0:T(4,128)S(1)}, u32[]{:S(2)}, u32[]{:S(2)}) collective-permute-start(f32[8,3,256]{2,1,0:T(4,128)S(1)} %copy.303), channel_id=1, source_target_pairs={{2,0},{4,2},{6,4},{8,6},{10,8},{12,10},{14,12},{16,14},{18,16},{20... | collective-permute-start | bytes 73736 | tf_op jit(solution)/shard_map/ppermute | solution.py:21
  276.6 13.7 %collective-permute-start.10 = (f32[8,3,256]{2,1,0:T(4,128)S(1)}, f32[8,3,256]{2,1,0:T(4,128)S(1)}, u32[]{:S(2)}, u32[]{:S(2)}) collective-permute-start(f32[8,3,256]{2,1,0:T(4,128)S(1)} %copy.303), channel_id=1, source_target_pairs={{4,0},{6,2},{8,4},{10,6},{12,8},{14,10},{16,12},{18,14},{20,16},{2... | collective-permute-start | bytes 73736 | tf_op jit(solution)/shard_map/ppermute | solution.py:21
  290.3 1.9 collective-permute-start.11
  292.2 1.3 collective-permute-start.12
  293.6 32.1 %all_gather.15.stl_ref = f32[8,3,2048]{2,1,0:T(4,128)} all-gather(f32[8,3,128]{2,1,0:T(4,128)S(1)} %fusion.13), channel_id=1, replica_groups=mesh['seq'=16,'fsdp'=2] {'seq'}, dimensions={2}, use_global_device_ids=true | all-gather | bytes 208896 | tf_op jit(solution)/shard_map/all_gather | solution.py:346
  326.5 19.4 %shard_map.104 = (bf16[8,256,128]{2,1,0:T(8,128)(2,1)}, bf16[8,256,128]{2,1,0:T(8,128)(2,1)}) custom-call(bf16[2,8,256,128]{3,2,1,0:T(8,128)(2,1)} %pad_maximum_fusion.2.k_ref.v_ref, bf16[2,8,256,128]{3,2,1,0:T(8,128)(2,1)} %pad_maximum_fusion.2.k_ref.v_ref, bf16[2,8,1280,128]{3,2,1,0:T(8,128)(2,1)} %constant_dynamic-update-slice_fusion.15.qs_ref.gs_ref, ...), custom_call_target="tpu_custom_call" | custom-call | tf_op jit(solution)/shard_map/pallas_call | solution.py:225
  345.9 1.5 select_bitcast_fusion.9
  348.8 1.5 bitcast_select_fusion.7
  350.5 1.3 reshape.952
  351.8 1.4 pad_maximum_fusion.4
  354.4 2.3 reshape.954
  356.7 1.3 pad_maximum_fusion.5
  359.2 2.3 reshape.956
  (160 shorter events, 27.8 us)
Async XLA Ops:
  7.2 46.5 %copy-start = (bf16[1,512,2048]{2,1,0:T(8,128)(2,1)S(1)}, bf16[1,512,2048]{2,1,0:T(8,128)(2,1)}, u32[]{:S(2)}) copy-start(bf16[1,512,2048]{2,1,0:T(8,128)(2,1)} %param.11) | copy-start | bytes 6291460
  7.2 37.1 %all-gather.4.cloned.1.call-start = ((), (), s32[]{:S(2)}) async-start(), calls=%async_computation | async-start | bytes 3145728 | tf_op jit(solution)/shard_map/all_gather | solution.py:284
  9.7 210.8 %all-gather.6.cloned.1.call-start = ((), (), s32[]{:S(2)}) async-start(), calls=%async_computation.1 | async-start | bytes 8912896 | tf_op jit(solution)/shard_map/all_gather | solution.py:270
  44.3 12.3 %collective-permute-start = (bf16[1024,1024]{1,0:T(8,128)(2,1)}, bf16[1024,1024]{1,0:T(8,128)(2,1)}, u32[]{:S(2)}, u32[]{:S(2)}) collective-permute-start(bf16[1024,1024]{1,0:T(8,128)(2,1)} %all-gather.4.cloned.1.call-done), channel_id=1, source_target_pairs={{0,2},{2,0},{4,6},{6,4},{8,10},{10,8},{12,14},{14,12},{16,18},{18,... | collective-permute-start | bytes 6291464 | tf_op jit(solution)/shard_map/ppermute | solution.py:290
  45.1 2.6 copy-start.19
  46.8 0.8 copy-start.2
  46.8 1.0 copy-start.4
  48.0 5.6 %copy-start.22 = (s32[8]{0:T(128)S(1)}, s32[8]{0:T(128)}, u32[]{:S(2)}) copy-start(s32[8]{0:T(128)} %param.13) | copy-start | bytes 100
  49.9 1.9 copy-start.10
  49.9 2.8 copy-start.11
  49.9 2.8 copy-start.9
  49.9 2.8 copy-start.12
  56.6 4.4 %copy-start.13 = (bf16[8,256,1,128]{3,1,0,2:T(8,128)(2,1)S(1)}, bf16[8,256,1,128]{3,1,0,2:T(8,128)(2,1)}, u32[]{:S(2)}) copy-start(bf16[8,256,1,128]{3,1,0,2:T(8,128)(2,1)} %copy.335) | copy-start | bytes 1572868
  56.6 4.4 %copy-start.14 = (bf16[8,256,1,128]{3,1,0,2:T(8,128)(2,1)S(1)}, bf16[8,256,1,128]{3,1,0,2:T(8,128)(2,1)}, u32[]{:S(2)}) copy-start(bf16[8,256,1,128]{3,1,0,2:T(8,128)(2,1)} %copy.334) | copy-start | bytes 1572868
  56.6 4.4 %copy-start.15 = (bf16[8,256,1,128]{3,1,0,2:T(8,128)(2,1)S(1)}, bf16[8,256,1,128]{3,1,0,2:T(8,128)(2,1)}, u32[]{:S(2)}) copy-start(bf16[8,256,1,128]{3,1,0,2:T(8,128)(2,1)} %copy.333) | copy-start | bytes 1572868
  56.6 4.4 %copy-start.16 = (bf16[8,256,1,128]{3,1,0,2:T(8,128)(2,1)S(1)}, bf16[8,256,1,128]{3,1,0,2:T(8,128)(2,1)}, u32[]{:S(2)}) copy-start(bf16[8,256,1,128]{3,1,0,2:T(8,128)(2,1)} %copy.332) | copy-start | bytes 1572868
  60.0 0.8 copy-start.7
  60.0 1.0 copy-start.6
  61.0 3.6 copy-start.23
  61.0 7.7 %copy-start.3 = (bf16[8,256,1,128]{3,0,2,1:T(8,128)(2,1)S(1)}, bf16[8,256,1,128]{3,0,2,1:T(8,128)(2,1)}, u32[]{:S(2)}) copy-start(bf16[8,256,1,128]{3,0,2,1:T(8,128)(2,1)} %copy-done.2) | copy-start | bytes 1572868
  61.0 7.7 %copy-start.5 = (bf16[8,256,1,128]{3,0,2,1:T(8,128)(2,1)S(1)}, bf16[8,256,1,128]{3,0,2,1:T(8,128)(2,1)}, u32[]{:S(2)}) copy-start(bf16[8,256,1,128]{3,0,2,1:T(8,128)(2,1)} %copy-done.4) | copy-start | bytes 1572868
  63.2 262.6 %all-gather.8.cloned.1.call-start = ((), (), s32[]{:S(2)}) async-start(), calls=%async_computation.2 | async-start | bytes 8912896 | tf_op jit(solution)/shard_map/all_gather | solution.py:270
  72.6 20.0 %copy-start.17 = (bf16[1,8,256,128]{3,2,1,0:T(8,128)(2,1)S(1)}, bf16[1,8,256,128]{3,2,1,0:T(8,128)(2,1)}, u32[]{:S(2)}) copy-start(bf16[1,8,256,128]{3,2,1,0:T(8,128)(2,1)} %get-tuple-element.108) | copy-start | bytes 1572868
  74.5 40.7 %collective-permute-start.1 = (bf16[2,8,256,128]{3,2,1,0:T(8,128)(2,1)}, bf16[2,8,256,128]{3,2,1,0:T(8,128)(2,1)}, u32[]{:S(2)}, u32[]{:S(2)}) collective-permute-start(bf16[2,8,256,128]{3,2,1,0:T(8,128)(2,1)} %get-tuple-element.25), channel_id=1, source_target_pairs={{0,2},{2,4},{4,6},{6,8},{8,10},{10,12},{12,14},{14,16},{16,18},{18... | collective-permute-start | bytes 3145736 | tf_op jit(solution)/shard_map/ppermute | solution.py:21
  77.5 97.2 %collective-permute-start.2 = (bf16[2,8,256,128]{3,2,1,0:T(8,128)(2,1)}, bf16[2,8,256,128]{3,2,1,0:T(8,128)(2,1)}, u32[]{:S(2)}, u32[]{:S(2)}) collective-permute-start(bf16[2,8,256,128]{3,2,1,0:T(8,128)(2,1)} %get-tuple-element.25), channel_id=1, source_target_pairs={{0,4},{2,6},{4,8},{6,10},{8,12},{10,14},{12,16},{14,18},{16,20},{1... | collective-permute-start | bytes 3145736 | tf_op jit(solution)/shard_map/ppermute | solution.py:21
  80.7 100.7 %collective-permute-start.3 = (bf16[2,8,256,128]{3,2,1,0:T(8,128)(2,1)}, bf16[2,8,256,128]{3,2,1,0:T(8,128)(2,1)}, u32[]{:S(2)}, u32[]{:S(2)}) collective-permute-start(bf16[2,8,256,128]{3,2,1,0:T(8,128)(2,1)} %get-tuple-element.25), channel_id=1, source_target_pairs={{0,6},{2,8},{4,10},{6,12},{8,14},{10,16},{12,18},{14,20},{16,22},{... | collective-permute-start | bytes 3145736 | tf_op jit(solution)/shard_map/ppermute | solution.py:21
  84.8 91.8 %copy-start.8 = (bf16[2,8,128,128]{3,2,1,0:T(8,128)(2,1)S(1)}, bf16[2,8,128,128]{3,2,1,0:T(8,128)(2,1)}, u32[]{:S(2)}) copy-start(bf16[2,8,128,128]{3,2,1,0:T(8,128)(2,1)} %get-tuple-element.24) | copy-start | bytes 1572868
  87.5 89.1 %copy-start.18 = (bf16[2,8,128,128]{3,2,1,0:T(8,128)(2,1)S(1)}, bf16[2,8,128,128]{3,2,1,0:T(8,128)(2,1)}, u32[]{:S(2)}) copy-start(bf16[2,8,128,128]{3,2,1,0:T(8,128)(2,1)} %get-tuple-element.23) | copy-start | bytes 1572868
  89.5 112.1 %collective-permute-start.4 = (bf16[2,8,256,128]{3,2,1,0:T(8,128)(2,1)}, bf16[2,8,256,128]{3,2,1,0:T(8,128)(2,1)S(1)}, u32[]{:S(2)}, u32[]{:S(2)}) collective-permute-start(bf16[2,8,256,128]{3,2,1,0:T(8,128)(2,1)} %get-tuple-element.25), channel_id=1, source_target_pairs={{0,8},{2,10},{4,12},{6,14},{8,16},{10,18},{12,20},{14,22},{16,24},... | collective-permute-start | bytes 3145736 | tf_op jit(solution)/shard_map/ppermute | solution.py:21
  95.0 107.8 %collective-permute-start.5 = (bf16[2,8,256,128]{3,2,1,0:T(8,128)(2,1)S(1)}, bf16[2,8,256,128]{3,2,1,0:T(8,128)(2,1)S(1)}, u32[]{:S(2)}, u32[]{:S(2)}) collective-permute-start(bf16[2,8,256,128]{3,2,1,0:T(8,128)(2,1)S(1)} %get-tuple-element.21), channel_id=1, source_target_pairs={{2,0},{4,2},{6,4},{8,6},{10,8},{12,10},{14,12},{16,14},{18,16},{20... | collective-permute-start | bytes 3145736 | tf_op jit(solution)/shard_map/ppermute | solution.py:21
  115.1 88.8 %collective-permute-start.6 = (bf16[2,8,256,128]{3,2,1,0:T(8,128)(2,1)S(1)}, bf16[2,8,256,128]{3,2,1,0:T(8,128)(2,1)S(1)}, u32[]{:S(2)}, u32[]{:S(2)}) collective-permute-start(bf16[2,8,256,128]{3,2,1,0:T(8,128)(2,1)S(1)} %get-tuple-element.21), channel_id=1, source_target_pairs={{4,0},{6,2},{8,4},{10,6},{12,8},{14,10},{16,12},{18,14},{20,16},{2... | collective-permute-start | bytes 3145736 | tf_op jit(solution)/shard_map/ppermute | solution.py:21
  174.7 37.9 %collective-permute-start.7 = (bf16[2,8,256,128]{3,2,1,0:T(8,128)(2,1)S(1)}, bf16[2,8,256,128]{3,2,1,0:T(8,128)(2,1)S(1)}, u32[]{:S(2)}, u32[]{:S(2)}) collective-permute-start(bf16[2,8,256,128]{3,2,1,0:T(8,128)(2,1)S(1)} %get-tuple-element.21), channel_id=1, source_target_pairs={{6,0},{8,2},{10,4},{12,6},{14,8},{16,10},{18,12},{20,14},{22,16},{... | collective-permute-start | bytes 3145736 | tf_op jit(solution)/shard_map/ppermute | solution.py:21
  181.4 37.8 %collective-permute-start.8 = (bf16[2,8,256,128]{3,2,1,0:T(8,128)(2,1)S(1)}, bf16[2,8,256,128]{3,2,1,0:T(8,128)(2,1)S(1)}, u32[]{:S(2)}, u32[]{:S(2)}) collective-permute-start(bf16[2,8,256,128]{3,2,1,0:T(8,128)(2,1)S(1)} %get-tuple-element.21), channel_id=1, source_target_pairs={{8,0},{10,2},{12,4},{14,6},{16,8},{18,10},{20,12},{22,14},{24,16},... | collective-permute-start | bytes 3145736 | tf_op jit(solution)/shard_map/ppermute | solution.py:21
  250.7 75.0 %collective-permute-start.9 = (f32[8,3,256]{2,1,0:T(4,128)S(1)}, f32[8,3,256]{2,1,0:T(4,128)S(1)}, u32[]{:S(2)}, u32[]{:S(2)}) collective-permute-start(f32[8,3,256]{2,1,0:T(4,128)S(1)} %copy.303), channel_id=1, source_target_pairs={{2,0},{4,2},{6,4},{8,6},{10,8},{12,10},{14,12},{16,14},{18,16},{20... | collective-permute-start | bytes 73736 | tf_op jit(solution)/shard_map/ppermute | solution.py:21
  276.6 49.1 %collective-permute-start.10 = (f32[8,3,256]{2,1,0:T(4,128)S(1)}, f32[8,3,256]{2,1,0:T(4,128)S(1)}, u32[]{:S(2)}, u32[]{:S(2)}) collective-permute-start(f32[8,3,256]{2,1,0:T(4,128)S(1)} %copy.303), channel_id=1, source_target_pairs={{4,0},{6,2},{8,4},{10,6},{12,8},{14,10},{16,12},{18,14},{20,16},{2... | collective-permute-start | bytes 73736 | tf_op jit(solution)/shard_map/ppermute | solution.py:21
  290.3 35.5 %collective-permute-start.11 = (f32[8,3,256]{2,1,0:T(4,128)S(1)}, f32[8,3,256]{2,1,0:T(4,128)S(1)}, u32[]{:S(2)}, u32[]{:S(2)}) collective-permute-start(f32[8,3,256]{2,1,0:T(4,128)S(1)} %copy.303), channel_id=1, source_target_pairs={{6,0},{8,2},{10,4},{12,6},{14,8},{16,10},{18,12},{20,14},{22,16},{... | collective-permute-start | bytes 73736 | tf_op jit(solution)/shard_map/ppermute | solution.py:21
  292.2 33.6 %collective-permute-start.12 = (f32[8,3,256]{2,1,0:T(4,128)S(1)}, f32[8,3,256]{2,1,0:T(4,128)S(1)}, u32[]{:S(2)}, u32[]{:S(2)}) collective-permute-start(f32[8,3,256]{2,1,0:T(4,128)S(1)} %copy.303), channel_id=1, source_target_pairs={{8,0},{10,2},{12,4},{14,6},{16,8},{18,10},{20,12},{22,14},{24,16},... | collective-permute-start | bytes 73736 | tf_op jit(solution)/shard_map/ppermute | solution.py:21
  325.8 0.7 copy-start.21
  325.8 20.1 %copy-start.20 = (bf16[8,256,128]{2,1,0:T(8,128)(2,1)S(1)}, bf16[8,256,128]{2,1,0:T(8,128)(2,1)}, u32[]{:S(2)}) copy-start(bf16[8,256,128]{2,1,0:T(8,128)(2,1)} %get-tuple-element.9) | copy-start | bytes 1572868
  351.8 9.7 %copy-start.1 = (bf16[1,512,2048]{2,1,0:T(8,128)(2,1)S(1)}, bf16[1,512,2048]{2,1,0:T(8,128)(2,1)}, u32[]{:S(2)}) copy-start(bf16[1,512,2048]{2,1,0:T(8,128)(2,1)} %param.11) | copy-start | bytes 6291460
Sparse Core Ops, SparseCore 0:
  10.1 34.1 all-gather.3
  63.4 141.2 all-gather.5
  206.8 81.3 all-gather.7

commit v5 on v4

--- a/solution.py
+++ b/solution.py
@@ -83,13 +83,6 @@
         shard_index * tok_dev
         + stride * jnp.arange(row_count, dtype=jnp.int32)[None, :]
         + offset[:, None]
-    )
-
-
-def window_positions(shard_index, distances, tok_dev, stride, offset, row_count):
-    return jnp.concatenate(
-        [row_positions(shard_index + d, tok_dev, stride, offset, row_count) for d in distances],
-        axis=1,
     )
 
 
@@ -137,19 +130,21 @@
     return grad_query, top, inverse, delta
 
 
-def query_kernel(
-    q_ref, g_ref, ks_ref, vs_ref, kl_ref, vl_ref,
-    qpos_ref, qss_ref, qsl_ref, kps_ref, kss_ref, kpl_ref, ksl_ref,
-    dq_ref, top_ref, inv_ref, delta_ref, *, scale,
-):
+def query_kernel(*refs, scale, n_short):
+    q_ref, g_ref, qpos_ref, qss_ref, qsl_ref = refs[:5]
+    shorts = [refs[5 + 4 * i : 9 + 4 * i] for i in range(n_short)]
+    kl_ref, vl_ref, kpl_ref, ksl_ref = refs[5 + 4 * n_short : 9 + 4 * n_short]
+    dq_ref, top_ref, inv_ref, delta_ref = refs[9 + 4 * n_short :]
     half = q_ref.shape[1] // 2
-    ks = ks_ref[0]
-    vs = vs_ref[0]
     for lo, hi, with_long in ((0, half, True), (half, 2 * half, False)):
         q = q_ref[0, lo:hi, :]
         g = g_ref[0, lo:hi, :]
         qpos = qpos_ref[0, lo:hi, :]
-        parts = [(ks, vs, (kps_ref[0] <= qpos) & (kss_ref[0] == qss_ref[0, lo:hi, :]))]
+        qseg = qss_ref[0, lo:hi, :]
+        parts = [
+            (ks_ref[0], vs_ref[0], (kps_ref[0] <= qpos) & (kss_ref[0] == qseg))
+            for ks_ref, vs_ref, kps_ref, kss_ref in shorts
+        ]
         if with_long:
             parts.append(
                 (kl_ref[0], vl_ref[0], (kpl_ref[0] <= qpos) & (ksl_ref[0] == qsl_ref[0, lo:hi, :]))
@@ -176,20 +171,21 @@
     return grad_key, grad_value
 
 
-def key_kernel(
-    k_ref, v_ref, qs_ref, gs_ref, ql_ref, gl_ref,
-    kpos_ref, kss_ref, ksl_ref, qps_ref, qss_ref, sts_ref, qpl_ref, qsl_ref, stl_ref,
-    dk_ref, dv_ref, *, scale,
-):
+def key_kernel(*refs, scale, n_short):
+    k_ref, v_ref, kpos_ref, kss_ref, ksl_ref = refs[:5]
+    shorts = [refs[5 + 5 * i : 10 + 5 * i] for i in range(n_short)]
+    ql_ref, gl_ref, qpl_ref, qsl_ref, stl_ref = refs[5 + 5 * n_short : 10 + 5 * n_short]
+    dk_ref, dv_ref = refs[10 + 5 * n_short :]
     half = k_ref.shape[1] // 2
-    qs = qs_ref[0]
-    gs = gs_ref[0]
-    sts = sts_ref[0]
     for lo, hi, with_long in ((0, half, True), (half, 2 * half, False)):
         k = k_ref[0, lo:hi, :]
         v = v_ref[0, lo:hi, :]
         kpos = kpos_ref[0, lo:hi, :]
-        parts = [(qs, gs, (kpos <= qps_ref[0]) & (kss_ref[0, lo:hi, :] == qss_ref[0]), sts)]
+        kseg = kss_ref[0, lo:hi, :]
+        parts = [
+            (qs_ref[0], gs_ref[0], (kpos <= qps_ref[0]) & (kseg == qss_ref[0]), sts_ref[0])
+            for qs_ref, gs_ref, qps_ref, qss_ref, sts_ref in shorts
+        ]
         if with_long:
             parts.append(
                 (
@@ -276,7 +272,6 @@
     own_kv = jnp.stack([split_rows(key_vectors[0]), split_rows(value_vectors[0])])
     all_kv_long = gathered(take_rows(own_kv, par_long))
     near_kv = [own_kv] + [passed_along(own_kv, "seq", d) for d in near_steps]
-    near_kv = jnp.concatenate(near_kv, axis=2)
 
     q_rows = split_rows(queries[0])
     core = shard_index % 2
@@ -304,37 +299,34 @@
     own_qg = jnp.stack([q_rows, g_rows])
     all_qg_long = gathered(take_rows(own_qg, par_long))
     near_qg = [own_qg] + [passed_along(own_qg, "seq", -d) for d in near_steps]
-    near_qg = jnp.concatenate(near_qg, axis=2)
 
     own_pos = row_positions(shard_index, tok_dev, 2, par_short, rows_short)
     own_seg_short = segment_of(own_pos, segments_short)
     own_is_long = (own_pos - head_phase[:, None]) % 4 == 0
     own_seg_long = jnp.where(own_is_long, segment_of(own_pos, segments_long), -3)
 
-    key_pos_short = window_positions(
-        shard_index, [-d for d in range(len(near_steps) + 1)], tok_dev, 2, par_short, rows_short
-    )
-    key_seg_short = jnp.where(key_pos_short >= 0, segment_of(key_pos_short, segments_short), -1)
+    short_keys = []
+    for d, window in enumerate(near_kv):
+        key_pos = row_positions(shard_index - d, tok_dev, 2, par_short, rows_short)
+        key_seg = jnp.where(key_pos >= 0, segment_of(key_pos, segments_short), -1)
+        short_keys += [(window, 0), (window, 1), row(key_pos), row(key_seg)]
+    ordered_pos = column(order_last(own_pos, par_long))
+    ordered_seg_short = column(order_last(own_seg_short, par_long))
+    ordered_seg_long = column(order_last(own_seg_long, par_long))
     f32 = jnp.float32
     row_shape = jax.ShapeDtypeStruct((head_count, rows_short, head_width), jnp.bfloat16)
     stat_shape = jax.ShapeDtypeStruct((head_count, rows_short, 1), f32)
     grad_query, top, inverse, delta = run_per_head(
-        functools.partial(query_kernel, scale=scale),
+        functools.partial(query_kernel, scale=scale, n_short=len(near_kv)),
         [
             order_rows(q_rows, par_long),
             order_rows(g_rows, par_long),
-            (near_kv, 0),
-            (near_kv, 1),
-            (all_kv_long, 0),
-            (all_kv_long, 1),
-            column(order_last(own_pos, par_long)),
-            column(order_last(own_seg_short, par_long)),
-            column(order_last(own_seg_long, par_long)),
-            row(key_pos_short),
-            row(key_seg_short),
-            row(long_pos),
-            row(long_seg),
-        ],
+            ordered_pos,
+            ordered_seg_short,
+            ordered_seg_long,
+        ]
+        + short_keys
+        + [(all_kv_long, 0), (all_kv_long, 1), row(long_pos), row(long_seg)],
         [row_shape, stat_shape, stat_shape, stat_shape],
     )
     grad_query = unorder_rows(grad_query, par_long)
@@ -342,35 +334,19 @@
         jnp.stack([top[:, :, 0], inverse[:, :, 0], delta[:, :, 0]], axis=1), par_long
     )
     near_stats = [own_stats] + [passed_along(own_stats, "seq", -d) for d in near_steps]
-    near_stats = jnp.concatenate(near_stats, axis=2)
     all_stats_long = lax.all_gather(take_stats(own_stats, par_long), "seq", axis=2, tiled=True)
 
-    query_pos_short = window_positions(
-        shard_index, list(range(len(near_steps) + 1)), tok_dev, 2, par_short, rows_short
-    )
-    query_seg_short = jnp.where(
-        query_pos_short < total, segment_of(query_pos_short, segments_short), -2
-    )
+    short_queries = []
+    for d, (window, stats) in enumerate(zip(near_qg, near_stats)):
+        query_pos = row_positions(shard_index + d, tok_dev, 2, par_short, rows_short)
+        query_seg = jnp.where(query_pos < total, segment_of(query_pos, segments_short), -2)
+        short_queries += [(window, 0), (window, 1), row(query_pos), row(query_seg), stats]
     ordered_kv = order_rows(own_kv, par_long)
     grad_key, grad_value = run_per_head(
-        functools.partial(key_kernel, scale=scale),
-        [
-            (ordered_kv, 0),
-            (ordered_kv, 1),
-            (near_qg, 0),
-            (near_qg, 1),
-            (all_qg_long, 0),
-            (all_qg_long, 1),
-            column(order_last(own_pos, par_long)),
-            column(order_last(own_seg_short, par_long)),
-            column(order_last(own_seg_long, par_long)),
-            row(query_pos_short),
-            row(query_seg_short),
-            near_stats,
-            row(long_pos),
-            row(long_seg),
-            all_stats_long,
-        ],
+        functools.partial(key_kernel, scale=scale, n_short=len(near_qg)),
+        [(ordered_kv, 0), (ordered_kv, 1), ordered_pos, ordered_seg_short, ordered_seg_long]
+        + short_queries
+        + [(all_qg_long, 0), (all_qg_long, 1), row(long_pos), row(long_seg), all_stats_long],
         [row_shape, row_shape],
     )
     grad_key = unorder_rows(grad_key, par_long)

time: 374 us -> 340 us (0.909)
  the two profiles are of different devices: /device:TPU:5 before, /device:TPU:0 now
where the time goes in v5:
time: 340 us; the launch traced here: 339 us
  waiting for transfers between devices  149 us (44%)
  Pallas kernels  50.6 us (15%)
  blocking collectives  49.3 us (14%)
  starting transfers between devices  24.6 us (7%)
  local copies, waits for them, and re-layouts  22.1 us (6%)
  other arithmetic  22.1 us (6%)
  between operations  15.3 us (4%)
  matrix products  5.78 us (2%)
    ppermute x12, waiting for transfers between devices, passed_along(): return lax.ppermute(value, axis, pairs)  82.4 us
    pallas_call x2, Pallas kernels, run_per_head(): pl.pallas_call(kernel, grid=(heads,), in_specs=list(specs), out_specs=[pe...  50.6 us
    all_gather x1, blocking collectives, shards(): lax.all_gather(take_stats(own_stats, par_long), 'seq', axis=2, tiled=True)  49.3 us
    all_gather x1, waiting for transfers between devices, shards(): lax.all_gather(lax.dynamic_slice_in_dim(out_weight, core * half_width, ha...  36.2 us
    all_gather x2, waiting for transfers between devices, gathered(): return lax.all_gather(tensor, 'seq', axis=2, tiled=True)  30.1 us
    ppermute x12, starting transfers between devices, passed_along(): return lax.ppermute(value, axis, pairs)  24.5 us
    unnamed x80, local copies, waits for them, and re-layouts  9.06 us
    select_n x5, other arithmetic, take_rows(): jnp.where((parity == 0)[:, None, None], paired[..., 0, :], paired[..., 1,...  7.36 us
  transfers between devices with their start and end apart: 16, of which 5 were waited for; matrix products, arithmetic and copies ran while one was open for 8% of the time, Pallas kernels for 7%

profile of v5, /device:TPU:0, one launch (start us, length us, event | category | flops | bytes accessed | tf_op | source)
XLA Modules:
  0.0 339.2 jit_solution(15016810007990720148)
XLA Ops:
  7.3 2.5 constant_dynamic-slice_fusion
  9.8 36.2 %all-gather.4.cloned.1.call-done = bf16[1024,1024]{1,0:T(8,128)(2,1)} async-done(((bf16[512,1024]{1,0:T(8,128)(2,1)}), bf16[1024,1024]{1,0:T(8,128)(2,1)}) %all-gather.4.cloned.1.call-update) | async-done | bytes 2097168 | tf_op jit(solution)/shard_map/all_gather | solution.py:279
  46.5 1.3 copy-done.22
  48.9 1.0 copy.300
  49.9 0.9 copy.299
  50.8 0.9 copy.298
  51.7 0.9 copy.297
  52.7 2.9 fusion.2
  55.5 2.9 fusion
  59.0 0.8 copy-done.16
  61.4 1.4 broadcast_select_fusion
  65.2 0.9 compare_select_fusion
  66.8 3.6 %bitcast_select_fusion.5 = (bf16[1,8,256,128]{3,2,1,0:T(8,128)(2,1)}, bf16[1,8,256,128]{3,2,1,0:T(8,128)(2,1)S(1)}, bf16[1,8,256,128]{3,2,1,0:T(8,128)(2,1)}, bf16[1,8,256,128]{3,2,1,0:T(8,128)(2,1)S(1)}) fusion(pred[8]{0:T(512)(128)(4,1)S(1)} %broadcast_compare_fusion.3, bf16[8,256,1,128]{3,0,2,1:T(8,128)(2,1)S(1)} %copy-done.9, ...), kind=kLoop, calls=%fused_computation.38 | loop fusion | flops 1048576 | bytes 6291464 | tf_op jit(solution)/shard_map/jit(_where)/select_n | solution.py:27
  70.5 3.4 %collective-permute-start.1 = (bf16[2,8,256,128]{3,2,1,0:T(8,128)(2,1)S(1)}, bf16[2,8,256,128]{3,2,1,0:T(8,128)(2,1)}, u32[]{:S(2)}, u32[]{:S(2)}) collective-permute-start(bf16[2,8,256,128]{3,2,1,0:T(8,128)(2,1)S(1)} %pad_maximum_fusion.refs_5_.refs_6_), channel_id=1, source_target_pairs={{0,2},{2,4},{4,6},{6,8},{8,10},{10,12},{12,14},{14,16},{16,18},{18... | collective-permute-start | bytes 3145736 | tf_op jit(solution)/shard_map/ppermute | solution.py:21
  73.9 3.5 %collective-permute-start.2 = (bf16[2,8,256,128]{3,2,1,0:T(8,128)(2,1)S(1)}, bf16[2,8,256,128]{3,2,1,0:T(8,128)(2,1)}, u32[]{:S(2)}, u32[]{:S(2)}) collective-permute-start(bf16[2,8,256,128]{3,2,1,0:T(8,128)(2,1)S(1)} %pad_maximum_fusion.refs_5_.refs_6_), channel_id=1, source_target_pairs={{0,4},{2,6},{4,8},{6,10},{8,12},{10,14},{12,16},{14,18},{16,20},{1... | collective-permute-start | bytes 3145736 | tf_op jit(solution)/shard_map/ppermute | solution.py:21
  77.4 3.7 %collective-permute-start.3 = (bf16[2,8,256,128]{3,2,1,0:T(8,128)(2,1)S(1)}, bf16[2,8,256,128]{3,2,1,0:T(8,128)(2,1)}, u32[]{:S(2)}, u32[]{:S(2)}) collective-permute-start(bf16[2,8,256,128]{3,2,1,0:T(8,128)(2,1)S(1)} %pad_maximum_fusion.refs_5_.refs_6_), channel_id=1, source_target_pairs={{0,6},{2,8},{4,10},{6,12},{8,14},{10,16},{12,18},{14,20},{16,22},{... | collective-permute-start | bytes 3145736 | tf_op jit(solution)/shard_map/ppermute | solution.py:21
  81.1 1.3 copy.246.refs_2_
  82.4 1.3 copy.247.refs_3_
  83.8 0.7 compare_convert_fusion.refs_28_.refs_33_
  84.5 3.4 %collective-permute-start.4 = (bf16[2,8,256,128]{3,2,1,0:T(8,128)(2,1)S(1)}, bf16[2,8,256,128]{3,2,1,0:T(8,128)(2,1)}, u32[]{:S(2)}, u32[]{:S(2)}) collective-permute-start(bf16[2,8,256,128]{3,2,1,0:T(8,128)(2,1)S(1)} %pad_maximum_fusion.refs_5_.refs_6_), channel_id=1, source_target_pairs={{0,8},{2,10},{4,12},{6,14},{8,16},{10,18},{12,20},{14,22},{16,24},... | collective-permute-start | bytes 3145736 | tf_op jit(solution)/shard_map/ppermute | solution.py:21
  87.9 1.3 copy.248.refs_4_
  89.3 1.3 pad_maximum_fusion.3.refs_5_.refs_6_
  90.6 1.3 collective-permute-start.5
  91.9 1.5 copy_select_fusion.4
  93.5 1.3 collective-permute-start.7
  94.8 19.5 %collective-permute-done.2.refs_13_.refs_14_ = bf16[2,8,256,128]{3,2,1,0:T(8,128)(2,1)} collective-permute-done((bf16[2,8,256,128]{3,2,1,0:T(8,128)(2,1)S(1)}, bf16[2,8,256,128]{3,2,1,0:T(8,128)(2,1)}, u32[]{:S(2)}, u32[]{:S(2)}) %collective-permute-start.2) | collective-permute-done | bytes 1048608 | tf_op jit(solution)/shard_map/ppermute | solution.py:21
  114.3 1.3 collective-permute-start.9
  115.5 62.9 %collective-permute-done.3.refs_17_.refs_18_ = bf16[2,8,256,128]{3,2,1,0:T(8,128)(2,1)} collective-permute-done((bf16[2,8,256,128]{3,2,1,0:T(8,128)(2,1)S(1)}, bf16[2,8,256,128]{3,2,1,0:T(8,128)(2,1)}, u32[]{:S(2)}, u32[]{:S(2)}) %collective-permute-start.3) | collective-permute-done | bytes 1048608 | tf_op jit(solution)/shard_map/ppermute | solution.py:21
  178.5 1.5 collective-permute-start.11
  180.1 1.1 pad_maximum_fusion.2.refs_0_.refs_1_
  181.2 1.1 pad_maximum_fusion.8
  182.3 19.7 %all-gather.6.cloned.1.call-done.refs_25_.refs_26_ = bf16[2,8,2048,128]{3,2,1,0:T(8,128)(2,1)} async-done(((bf16[2,8,128,128]{3,2,1,0:T(8,128)(2,1)}), bf16[2,8,2048,128]{3,2,1,0:T(8,128)(2,1)}) %all-gather.6.cloned.1.call-update) | async-done | bytes 8388624 | tf_op jit(solution)/shard_map/all_gather | solution.py:266
  202.0 24.6 %shard_map.103 = (bf16[8,256,128]{2,1,0:T(8,128)(2,1)}, f32[8,256,1]{2,1,0:T(8,128)}, f32[8,256,1]{2,1,0:T(8,128)}, f32[8,256,1]{2,1,0:T(8,128)}) custom-call(bf16[8,256,128]{2,1,0:T(8,128)(2,1)} %get-tuple-element.155.refs_0_, bf16[8,256,128]{2,1,0:T(8,128)(2,1)} %get-tuple-element.156.refs_1_, s32[8,256,1]{2,1,0:T(8,128)} %copy.246.refs_2_, ...), custom_call_target="tpu_custom_call" | custom-call | tf_op jit(solution)/shard_map/pallas_call | solution.py:221
  226.6 1.7 reduce.2
  228.2 1.6 reduce.1
  230.7 1.3 collective-permute-start.6
  232.1 1.3 collective-permute-start.8
  233.4 1.3 collective-permute-start.10
  234.7 1.3 collective-permute-start.12
  236.0 49.3 %all_gather.15.refs_34_ = f32[8,3,2048]{2,1,0:T(4,128)} all-gather(f32[8,3,128]{2,1,0:T(4,128)S(1)} %fusion.13), channel_id=1, replica_groups=mesh['seq'=16,'fsdp'=2] {'seq'}, dimensions={2}, use_global_device_ids=true | all-gather | bytes 208896 | tf_op jit(solution)/shard_map/all_gather | solution.py:337
  285.3 10.5 %all-gather.8.cloned.1.call-done.refs_30_.refs_31_ = bf16[2,8,2048,128]{3,2,1,0:T(8,128)(2,1)} async-done(((bf16[2,8,128,128]{3,2,1,0:T(8,128)(2,1)}), bf16[2,8,2048,128]{3,2,1,0:T(8,128)(2,1)}) %all-gather.8.cloned.1.call-update) | async-done | bytes 8388624 | tf_op jit(solution)/shard_map/all_gather | solution.py:266
  296.4 26.0 %shard_map.104 = (bf16[8,256,128]{2,1,0:T(8,128)(2,1)}, bf16[8,256,128]{2,1,0:T(8,128)(2,1)}) custom-call(bf16[2,8,256,128]{3,2,1,0:T(8,128)(2,1)} %pad_maximum_fusion.2.refs_0_.refs_1_, bf16[2,8,256,128]{3,2,1,0:T(8,128)(2,1)} %pad_maximum_fusion.2.refs_0_.refs_1_, s32[8,256,1]{2,1,0:T(8,128)} %copy.246.refs_2_, s32[8,256,1]{2,1,0:T(8,128)} %copy.247.refs_3_, ...), custom_call_target="tpu_custom_call" | custom-call | tf_op jit(solution)/shard_map/pallas_call | solution.py:221
  322.5 1.5 select_bitcast_fusion.9
  325.3 1.3 bitcast_select_fusion.7
  326.8 1.3 reshape.1541
  328.1 1.3 pad_maximum_fusion.4
  329.6 1.3 reshape.1543
  331.2 1.3 reshape.1545
  (140 shorter events, 10.1 us)
Async XLA Ops:
  7.2 45.5 %copy-start = (bf16[1,512,2048]{2,1,0:T(8,128)(2,1)S(1)}, bf16[1,512,2048]{2,1,0:T(8,128)(2,1)}, u32[]{:S(2)}) copy-start(bf16[1,512,2048]{2,1,0:T(8,128)(2,1)} %param.11) | copy-start | bytes 6291460
  7.2 38.8 %copy-start.21 = (bf16[1,512,1024]{2,1,0:T(8,128)(2,1)S(1)}, bf16[1,512,1024]{2,1,0:T(8,128)(2,1)}, u32[]{:S(2)}) copy-start(bf16[1,512,1024]{2,1,0:T(8,128)(2,1)} %param.8) | copy-start | bytes 3145732
  7.2 38.8 %all-gather.4.cloned.1.call-start = ((), (), s32[]{:S(2)}) async-start(), calls=%async_computation | async-start | bytes 3145728 | tf_op jit(solution)/shard_map/all_gather | solution.py:279
  9.7 192.2 %all-gather.6.cloned.1.call-start = ((), (), s32[]{:S(2)}) async-start(), calls=%async_computation.1 | async-start | bytes 8912896 | tf_op jit(solution)/shard_map/all_gather | solution.py:266
  46.0 9.6 %collective-permute-start = (bf16[1024,1024]{1,0:T(8,128)(2,1)}, bf16[1024,1024]{1,0:T(8,128)(2,1)}, u32[]{:S(2)}, u32[]{:S(2)}) collective-permute-start(bf16[1024,1024]{1,0:T(8,128)(2,1)} %all-gather.4.cloned.1.call-done), channel_id=1, source_target_pairs={{0,2},{2,0},{4,6},{6,4},{8,10},{10,8},{12,14},{14,12},{16,18},{18,... | collective-permute-start | bytes 6291464 | tf_op jit(solution)/shard_map/ppermute | solution.py:285
  46.2 1.6 copy-start.22
  46.3 1.8 copy-start.6
  46.3 1.8 copy-start.8
  46.4 1.8 copy-start.23
  48.8 2.0 copy-start.12
  48.8 2.9 copy-start.13
  48.8 2.9 copy-start.11
  48.8 2.8 copy-start.14
  48.9 3.7 %copy-start.31 = (s32[8]{0:T(128)S(1)}, s32[8]{0:T(128)}, u32[]{:S(2)}) copy-start(s32[8]{0:T(128)} %param.13) | copy-start | bytes 100
  58.7 1.0 copy-start.16
  58.7 1.5 copy-start.17
  58.8 1.7 copy-start.18
  58.8 1.9 copy-start.19
  58.9 2.4 copy-start.4
  59.0 2.3 copy-start.5
  61.4 2.8 copy-start.32
  62.8 4.0 %copy-start.7 = (bf16[8,256,1,128]{3,0,2,1:T(8,128)(2,1)S(1)}, bf16[8,256,1,128]{3,0,2,1:T(8,128)(2,1)}, u32[]{:S(2)}) copy-start(bf16[8,256,1,128]{3,0,2,1:T(8,128)(2,1)} %copy-done.6) | copy-start | bytes 1572868
  62.8 4.0 %copy-start.9 = (bf16[8,256,1,128]{3,0,2,1:T(8,128)(2,1)S(1)}, bf16[8,256,1,128]{3,0,2,1:T(8,128)(2,1)}, u32[]{:S(2)}) copy-start(bf16[8,256,1,128]{3,0,2,1:T(8,128)(2,1)} %copy-done.8) | copy-start | bytes 1572868
  62.8 232.9 %all-gather.8.cloned.1.call-start = ((), (), s32[]{:S(2)}) async-start(), calls=%async_computation.2 | async-start | bytes 8912896 | tf_op jit(solution)/shard_map/all_gather | solution.py:266
  70.5 20.1 %copy-start.3 = (bf16[2,8,256,128]{3,2,1,0:T(8,128)(2,1)}, bf16[2,8,256,128]{3,2,1,0:T(8,128)(2,1)S(1)}, u32[]{:S(2)}) copy-start(bf16[2,8,256,128]{3,2,1,0:T(8,128)(2,1)S(1)} %pad_maximum_fusion.refs_5_.refs_6_) | copy-start | bytes 3145732
  70.5 23.0 %collective-permute-start.1 = (bf16[2,8,256,128]{3,2,1,0:T(8,128)(2,1)S(1)}, bf16[2,8,256,128]{3,2,1,0:T(8,128)(2,1)}, u32[]{:S(2)}, u32[]{:S(2)}) collective-permute-start(bf16[2,8,256,128]{3,2,1,0:T(8,128)(2,1)S(1)} %pad_maximum_fusion.refs_5_.refs_6_), channel_id=1, source_target_pairs={{0,2},{2,4},{4,6},{6,8},{8,10},{10,12},{12,14},{14,16},{16,18},{18... | collective-permute-start | bytes 3145736 | tf_op jit(solution)/shard_map/ppermute | solution.py:21
  73.9 40.4 %collective-permute-start.2 = (bf16[2,8,256,128]{3,2,1,0:T(8,128)(2,1)S(1)}, bf16[2,8,256,128]{3,2,1,0:T(8,128)(2,1)}, u32[]{:S(2)}, u32[]{:S(2)}) collective-permute-start(bf16[2,8,256,128]{3,2,1,0:T(8,128)(2,1)S(1)} %pad_maximum_fusion.refs_5_.refs_6_), channel_id=1, source_target_pairs={{0,4},{2,6},{4,8},{6,10},{8,12},{10,14},{12,16},{14,18},{16,20},{1... | collective-permute-start | bytes 3145736 | tf_op jit(solution)/shard_map/ppermute | solution.py:21
  77.4 101.1 %collective-permute-start.3 = (bf16[2,8,256,128]{3,2,1,0:T(8,128)(2,1)S(1)}, bf16[2,8,256,128]{3,2,1,0:T(8,128)(2,1)}, u32[]{:S(2)}, u32[]{:S(2)}) collective-permute-start(bf16[2,8,256,128]{3,2,1,0:T(8,128)(2,1)S(1)} %pad_maximum_fusion.refs_5_.refs_6_), channel_id=1, source_target_pairs={{0,6},{2,8},{4,10},{6,12},{8,14},{10,16},{12,18},{14,20},{16,22},{... | collective-permute-start | bytes 3145736 | tf_op jit(solution)/shard_map/ppermute | solution.py:21
  84.5 97.8 %collective-permute-start.4 = (bf16[2,8,256,128]{3,2,1,0:T(8,128)(2,1)S(1)}, bf16[2,8,256,128]{3,2,1,0:T(8,128)(2,1)}, u32[]{:S(2)}, u32[]{:S(2)}) collective-permute-start(bf16[2,8,256,128]{3,2,1,0:T(8,128)(2,1)S(1)} %pad_maximum_fusion.refs_5_.refs_6_), channel_id=1, source_target_pairs={{0,8},{2,10},{4,12},{6,14},{8,16},{10,18},{12,20},{14,22},{16,24},... | collective-permute-start | bytes 3145736 | tf_op jit(solution)/shard_map/ppermute | solution.py:21
  90.6 89.5 %copy-start.2 = (bf16[2,8,256,128]{3,2,1,0:T(8,128)(2,1)}, bf16[2,8,256,128]{3,2,1,0:T(8,128)(2,1)S(1)}, u32[]{:S(2)}) copy-start(bf16[2,8,256,128]{3,2,1,0:T(8,128)(2,1)S(1)} %pad_maximum_fusion.3.refs_5_.refs_6_) | copy-start | bytes 3145732
  90.6 141.5 %collective-permute-start.5 = (bf16[2,8,256,128]{3,2,1,0:T(8,128)(2,1)S(1)}, bf16[2,8,256,128]{3,2,1,0:T(8,128)(2,1)}, u32[]{:S(2)}, u32[]{:S(2)}) collective-permute-start(bf16[2,8,256,128]{3,2,1,0:T(8,128)(2,1)S(1)} %pad_maximum_fusion.3.refs_5_.refs_6_), channel_id=1, source_target_pairs={{2,0},{4,2},{6,4},{8,6},{10,8},{12,10},{14,12},{16,14},{18,16},{20... | collective-permute-start | bytes 3145736 | tf_op jit(solution)/shard_map/ppermute | solution.py:21
  91.9 88.2 %copy-start.10 = (bf16[2,8,128,128]{3,2,1,0:T(8,128)(2,1)S(1)}, bf16[2,8,128,128]{3,2,1,0:T(8,128)(2,1)}, u32[]{:S(2)}) copy-start(bf16[2,8,128,128]{3,2,1,0:T(8,128)(2,1)} %get-tuple-element.29) | copy-start | bytes 1572868
  91.9 88.2 %copy-start.20 = (bf16[2,8,128,128]{3,2,1,0:T(8,128)(2,1)S(1)}, bf16[2,8,128,128]{3,2,1,0:T(8,128)(2,1)}, u32[]{:S(2)}) copy-start(bf16[2,8,128,128]{3,2,1,0:T(8,128)(2,1)} %get-tuple-element.28) | copy-start | bytes 1572868
  93.5 139.9 %collective-permute-start.7 = (bf16[2,8,256,128]{3,2,1,0:T(8,128)(2,1)S(1)}, bf16[2,8,256,128]{3,2,1,0:T(8,128)(2,1)S(1)}, u32[]{:S(2)}, u32[]{:S(2)}) collective-permute-start(bf16[2,8,256,128]{3,2,1,0:T(8,128)(2,1)S(1)} %pad_maximum_fusion.3.refs_5_.refs_6_), channel_id=1, source_target_pairs={{4,0},{6,2},{8,4},{10,6},{12,8},{14,10},{16,12},{18,14},{20,16},{2... | collective-permute-start | bytes 3145736 | tf_op jit(solution)/shard_map/ppermute | solution.py:21
  114.3 120.5 %collective-permute-start.9 = (bf16[2,8,256,128]{3,2,1,0:T(8,128)(2,1)S(1)}, bf16[2,8,256,128]{3,2,1,0:T(8,128)(2,1)}, u32[]{:S(2)}, u32[]{:S(2)}) collective-permute-start(bf16[2,8,256,128]{3,2,1,0:T(8,128)(2,1)S(1)} %pad_maximum_fusion.3.refs_5_.refs_6_), channel_id=1, source_target_pairs={{6,0},{8,2},{10,4},{12,6},{14,8},{16,10},{18,12},{20,14},{22,16},{... | collective-permute-start | bytes 3145736 | tf_op jit(solution)/shard_map/ppermute | solution.py:21
  178.5 106.8 %collective-permute-start.11 = (bf16[2,8,256,128]{3,2,1,0:T(8,128)(2,1)S(1)}, bf16[2,8,256,128]{3,2,1,0:T(8,128)(2,1)}, u32[]{:S(2)}, u32[]{:S(2)}) collective-permute-start(bf16[2,8,256,128]{3,2,1,0:T(8,128)(2,1)S(1)} %pad_maximum_fusion.3.refs_5_.refs_6_), channel_id=1, source_target_pairs={{8,0},{10,2},{12,4},{14,6},{16,8},{18,10},{20,12},{22,14},{24,16},... | collective-permute-start | bytes 3145736 | tf_op jit(solution)/shard_map/ppermute | solution.py:21
  226.5 3.3 copy-start.24
  230.7 65.1 %copy-start.26 = (f32[8,3,256]{2,1,0:T(4,128)}, f32[8,3,256]{2,1,0:T(4,128)S(1)}, u32[]{:S(2)}) copy-start(f32[8,3,256]{2,1,0:T(4,128)S(1)} %copy.270.refs_9_) | copy-start | bytes 73732
  230.7 65.0 %collective-permute-start.6 = (f32[8,3,256]{2,1,0:T(4,128)S(1)}, f32[8,3,256]{2,1,0:T(4,128)S(1)}, u32[]{:S(2)}, u32[]{:S(2)}) collective-permute-start(f32[8,3,256]{2,1,0:T(4,128)S(1)} %copy.270.refs_9_), channel_id=1, source_target_pairs={{2,0},{4,2},{6,4},{8,6},{10,8},{12,10},{14,12},{16,14},{18,16},{20... | collective-permute-start | bytes 73736 | tf_op jit(solution)/shard_map/ppermute | solution.py:21
  232.1 63.6 %collective-permute-start.8 = (f32[8,3,256]{2,1,0:T(4,128)S(1)}, f32[8,3,256]{2,1,0:T(4,128)S(1)}, u32[]{:S(2)}, u32[]{:S(2)}) collective-permute-start(f32[8,3,256]{2,1,0:T(4,128)S(1)} %copy.270.refs_9_), channel_id=1, source_target_pairs={{4,0},{6,2},{8,4},{10,6},{12,8},{14,10},{16,12},{18,14},{20,16},{2... | collective-permute-start | bytes 73736 | tf_op jit(solution)/shard_map/ppermute | solution.py:21
  233.4 62.4 %copy-start.15 = (bf16[2,8,256,128]{3,2,1,0:T(8,128)(2,1)}, bf16[2,8,256,128]{3,2,1,0:T(8,128)(2,1)S(1)}, u32[]{:S(2)}) copy-start(bf16[2,8,256,128]{3,2,1,0:T(8,128)(2,1)S(1)} %collective-permute-done.7.refs_15_.refs_16_) | copy-start | bytes 3145732
  233.4 62.3 %collective-permute-start.10 = (f32[8,3,256]{2,1,0:T(4,128)S(1)}, f32[8,3,256]{2,1,0:T(4,128)S(1)}, u32[]{:S(2)}, u32[]{:S(2)}) collective-permute-start(f32[8,3,256]{2,1,0:T(4,128)S(1)} %copy.270.refs_9_), channel_id=1, source_target_pairs={{6,0},{8,2},{10,4},{12,6},{14,8},{16,10},{18,12},{20,14},{22,16},{... | collective-permute-start | bytes 73736 | tf_op jit(solution)/shard_map/ppermute | solution.py:21
  234.7 61.0 %collective-permute-start.12 = (f32[8,3,256]{2,1,0:T(4,128)S(1)}, f32[8,3,256]{2,1,0:T(4,128)S(1)}, u32[]{:S(2)}, u32[]{:S(2)}) collective-permute-start(f32[8,3,256]{2,1,0:T(4,128)S(1)} %copy.270.refs_9_), channel_id=1, source_target_pairs={{8,0},{10,2},{12,4},{14,6},{16,8},{18,10},{20,12},{22,14},{24,16},... | collective-permute-start | bytes 73736 | tf_op jit(solution)/shard_map/ppermute | solution.py:21
  295.7 0.6 copy-start.27
  295.7 0.6 copy-start.28
  295.8 0.6 copy-start.29
  296.4 26.1 %copy-start.25 = (bf16[8,256,128]{2,1,0:T(8,128)(2,1)S(1)}, bf16[8,256,128]{2,1,0:T(8,128)(2,1)}, u32[]{:S(2)}) copy-start(bf16[8,256,128]{2,1,0:T(8,128)(2,1)} %get-tuple-element.9) | copy-start | bytes 1572868
  330.9 1.8 copy-start.1
  (1 other events, 0.6 us)
Sparse Core Ops, SparseCore 0:
  10.1 35.8 all-gather.3
  62.9 138.9 all-gather.5
  204.2 91.5 all-gather.7
